TPU v7x, 256 devices: a whole 4x4x8 slice. The times are simulated.
256 devices in a mesh: dp: 16 (over z_lo, x), tensor: 16 (over y, z_hi, core).
Axes of the slice: x: 4, y: 4, z: 8 (z_hi: 2, z_lo: 4; z = z_hi * 4 + z_lo), core: 2. Of those that a mesh axis runs over, the one named last changes fastest.
Arguments:
- inner_x: bfloat16 [16, 2048, 7168], P('dp', None, 'tensor')
- gate_z: bfloat16 [16, 2048, 7168], P('dp', None, 'tensor'), may hold values from -6 to 6
- input_b: bfloat16 [16, 2048, 128], P('dp'), may hold values from -0.75 to 0.75
- output_c: bfloat16 [16, 2048, 128], P('dp'), may hold values from -6 to 6
- step_raw: float32 [16, 2048, 112], P('dp', None, 'tensor'), may hold values from -6 to 6
- decay_rate: float32 [112], P('tensor'), may hold values from 0.001 to 0.05
- skip_gain: float32 [112], P('tensor'), may hold values from 0.5 to 1.5
- norm_gain: float32 [7168], P('tensor'), may hold values from 0.5 to 1.5
- out_weight: bfloat16 [7168, 3584], P('tensor'), may hold values from -0.0625 to 0.0625
- segment: int32 [16, 2048], P('dp'), may hold values from 0 to 7, never falling along the last dimension, each value on 1 to 1024 neighbouring positions
- cache_slot: int32 [16, 8], replicated, may hold values from 0 to 127, as said below
Outputs:
- mixed: bfloat16 [16, 2048, 3584], P('dp', 'tensor')
- cache: float32 [128, 112, 4096], P('dp', 'tensor')
Inputs may be any that keep to these rules, and one draw needn't show every extreme that they name: `segment`: in each group's row the prompt numbers never fall and every prompt 0 to 7 is present. `cache_slot`: every slot is named exactly once; slot // 8 is the owning group, and no two prompts of one group have the same owning group.
All inputs are finite; a program needn't handle non-finite values.
Results may differ from a plain program's by a relative error of at most 0.018.
Values may be sent and summed in bfloat16 or wider, within the bound.
No kernel may reach another device: no remote copies, remote signals or barrier semaphores. Data moves between devices by JAX's collectives and lax.ppermute only.
A program may use at most 192 MiB of HBM per device.

v0:
```python
import jax
import jax.numpy as jnp
from jax import lax
from jax.sharding import PartitionSpec as P

HEADS = 112
HEAD = 64
STATE = 64
NGROUPS = 2
REQS = 8
BLOCK = 256
INNER = 7168


HIGHEST = lax.Precision.HIGHEST


def split_pair(values):
    upper = values.astype(jnp.bfloat16)
    lower = (values - upper.astype(jnp.float32)).astype(jnp.bfloat16)
    return (upper, lower)


def split_einsum(form, wide, narrow):
    upper, lower = split_pair(wide)
    first = jnp.einsum(form, upper, narrow, preferred_element_type=jnp.float32)
    return first + jnp.einsum(form, lower, narrow, preferred_element_type=jnp.float32)


def local(
    inner_x,
    gate_z,
    input_b,
    output_c,
    step_raw,
    decay_rate,
    skip_gain,
    norm_gain,
    out_weight,
    segment,
    cache_slot,
):
    stream_len = inner_x.shape[1]
    dev_width = inner_x.shape[2]
    dev_heads = decay_rate.shape[0]
    tensor_idx = lax.axis_index("tensor")
    group_idx = tensor_idx * dev_heads // (HEADS // NGROUPS)
    b_cols = lax.dynamic_slice_in_dim(input_b[0], group_idx * STATE, STATE, 1)
    c_cols = lax.dynamic_slice_in_dim(output_c[0], group_idx * STATE, STATE, 1)
    step_size = jax.nn.softplus(step_raw[0])
    cum_log = jnp.cumsum(-decay_rate[None, :] * step_size, axis=0)
    seg_row = segment[0]
    block_count = stream_len // BLOCK
    prev_cum = jnp.concatenate([jnp.zeros((1, dev_heads), jnp.float32), cum_log[:-1]], axis=0)[
        ::BLOCK
    ]
    prev_seg = jnp.concatenate([jnp.full((1,), -1, seg_row.dtype), seg_row[:-1]], axis=0)[::BLOCK]
    block_inputs = (
        inner_x[0].reshape(block_count, BLOCK, dev_heads, HEAD),
        cum_log.reshape(block_count, BLOCK, dev_heads),
        step_size.reshape(block_count, BLOCK, dev_heads),
        seg_row.reshape(block_count, BLOCK),
        b_cols.reshape(block_count, BLOCK, STATE),
        c_cols.reshape(block_count, BLOCK, STATE),
        prev_cum,
        prev_seg,
    )
    positions = jnp.arange(BLOCK)

    def advance(carried, block_in):
        x_blk, cum_blk, step_blk, seg_blk, b_blk, c_blk, prev_c, prev_s = block_in
        scores = jnp.dot(c_blk, b_blk.T, preferred_element_type=jnp.float32)
        causal_mask = (positions[None, :] <= positions[:, None]) & (
            seg_blk[:, None] == seg_blk[None, :]
        )
        log_gap = cum_blk.T[:, :, None] - cum_blk.T[:, None, :]
        weights = (
            jnp.exp(jnp.where(causal_mask[None], log_gap, -jnp.inf))
            * step_blk.T[:, None, :]
            * scores[None]
        )
        intra_part = split_einsum("hts,shp->thp", weights, x_blk)
        live_rows = (seg_blk == prev_s).astype(jnp.float32)
        carry_decay = jnp.exp(cum_blk - prev_c[None, :]) * live_rows[:, None]
        carry_part = split_einsum("hpn,tn->thp", carried, c_blk) * carry_decay[:, :, None]
        outputs = intra_part + carry_part + skip_gain[None, :, None] * x_blk.astype(jnp.float32)
        last_seg = seg_blk[-1]
        last_cum = cum_blk[-1]
        keep_rows = (last_seg == prev_s).astype(jnp.float32)
        pull_back = (
            jnp.exp(last_cum[None, :] - cum_blk)
            * step_blk
            * (seg_blk == last_seg).astype(jnp.float32)[:, None]
        )
        added_part = split_einsum("shp,sn->hpn", pull_back[:, :, None] * x_blk, b_blk)
        carried = carried * (jnp.exp(last_cum - prev_c) * keep_rows)[:, None, None] + added_part
        return (carried, outputs)

    _, outputs = lax.scan(advance, jnp.zeros((dev_heads, HEAD, STATE), jnp.float32), block_inputs)
    mixer_y = outputs.reshape(stream_len, dev_width)
    members = (seg_row[None, :] == jnp.arange(REQS)[:, None]).astype(jnp.float32)
    end_index = (
        jnp.sum((seg_row[None, :] <= jnp.arange(REQS)[:, None]).astype(jnp.int32), axis=1) - 1
    )
    at_end = (jnp.arange(stream_len)[None, :] == end_index[:, None]).astype(jnp.float32)
    end_cum = jnp.dot(at_end, cum_log, precision=HIGHEST)
    seg_end_cum = jnp.dot(members.T, end_cum, precision=HIGHEST)
    pull_all = jnp.exp(seg_end_cum - cum_log) * step_size
    weighted = (inner_x[0].reshape(stream_len, dev_heads, HEAD) * pull_all[:, :, None]).reshape(
        stream_len, dev_width
    )
    masked_b = (
        (members.astype(jnp.bfloat16)[:, :, None] * b_cols[None])
        .transpose(1, 0, 2)
        .reshape(stream_len, REQS * STATE)
    )
    finals = split_einsum("tc,tk->ck", weighted, masked_b)
    finals = (
        finals.reshape(dev_heads, HEAD, REQS, STATE)
        .transpose(2, 0, 1, 3)
        .reshape(REQS, dev_heads * HEAD * STATE)
    )
    gated = mixer_y * jax.nn.silu(gate_z[0].astype(jnp.float32))
    sum_sq = jnp.sum(gated * gated, axis=1)
    group_hot = (jnp.arange(NGROUPS) == group_idx).astype(jnp.float32)
    group_stat = lax.psum(sum_sq[:, None] * group_hot[None, :], "tensor")
    mean_sq = jnp.sum(group_stat * group_hot[None, :], axis=1) / (INNER // NGROUPS)
    rounded = (gated * lax.rsqrt(mean_sq + 1e-05)[:, None] * norm_gain[None, :]).astype(
        jnp.bfloat16
    )
    projected = lax.psum_scatter(
        jnp.dot(rounded, out_weight, preferred_element_type=jnp.float32).astype(jnp.bfloat16),
        "tensor",
        scatter_dimension=0,
        tiled=True,
    )
    mixed = projected[None]
    dp_idx = lax.axis_index("dp")
    dp_size = lax.axis_size("dp")
    own_slots = lax.dynamic_slice_in_dim(cache_slot, dp_idx, 1, 0)[0]
    dest_hot = ((own_slots // REQS)[:, None] == jnp.arange(dp_size)[None, :]).astype(jnp.float32)
    outbound = jnp.dot(dest_hot.T, finals, precision=HIGHEST).reshape(
        dp_size, dev_heads, HEAD * STATE
    )
    inbound = lax.all_to_all(
        outbound.astype(jnp.bfloat16), "dp", split_axis=0, concat_axis=0, tiled=True
    ).astype(outbound.dtype)
    wanted = dp_idx * REQS + jnp.arange(REQS)
    take_hot = jnp.any(cache_slot[:, :, None] == wanted[None, None, :], axis=1).astype(jnp.float32)
    cache = jnp.dot(
        take_hot.T, inbound.reshape(dp_size, dev_heads * HEAD * STATE), precision=HIGHEST
    )
    return (mixed, cache.reshape(REQS, dev_heads, HEAD * STATE))


def solution(mesh):
    in_specs = (
        P("dp", None, "tensor"),
        P("dp", None, "tensor"),
        P("dp", None, None),
        P("dp", None, None),
        P("dp", None, "tensor"),
        P("tensor"),
        P("tensor"),
        P("tensor"),
        P("tensor", None),
        P("dp", None),
        P(),
    )
    out_specs = (P("dp", "tensor", None), P("dp", "tensor", None))
    return jax.shard_map(local, mesh=mesh, in_specs=in_specs, out_specs=out_specs, check_vma=False)
```

profile of v0, /device:TPU:32, one launch (start us, length us, event | category | flops | bytes accessed | tf_op | source)
XLA Modules:
  0.0 556.6 jit_solution(15308856619682689794)
XLA Ops:
  7.8 2.8 constant_dynamic-slice_fusion.3
  10.7 1.9 copy.77
  14.3 1.9 copy.65
  16.4 2.0 reduce-window.6
  21.2 2.1 copy.87
  23.3 1.7 copy.63
  25.0 1.6 reduce.4
  26.6 1.5 compare_select_fusion.1
  30.0 217.2 %while.13 = (s32[]{:T(128)}, f32[7,64,64]{2,1,0:T(8,128)S(1)}, f32[8,256,7,64]{1,0,3,2:T(8,128)}, f32[8,256,7]{1,2,0:T(8,128)S(1)}, f32[8,7]{1,0:T(8,128)S(1)}, ...) while((s32[]{:T(128)}, f32[7,64,64]{2,1,0:T(8,128)S(1)}, ...), condition=%wide.region_3.4_spmd.clone, body=%wide.region_2.3_spmd.clone.sunk | while | flops 192841488 | bytes 8220087 | solution.py:99
  30.7 1.3 dynamic_slice.129
  33.5 1.3 compare_convert_fusion.4
  38.8 1.6 fusion.151
  40.4 1.8 fusion.152
  43.5 11.3 %dynamic_update_slice.6 = f32[8,256,7,64]{1,0,3,2:T(8,128)} dynamic-update-slice(f32[8,256,7,64]{1,0,3,2:T(8,128)} %get-tuple-element.315, f32[1,256,7,64]{1,0,3,2:T(1,128)} %copy.140, s32[]{:T(128)} %get-tuple-element.313, s32[]{:T(128)} %constant.69.clone.1..sunk, s32[]{:T(128)} %constant.69.clone.1..sunk, s32[]{:T(128)} %constant.69.clone.1..sunk) | dynamic-update-slice | bytes 917508 | tf_op jit(solution)/shard_map/while/body/jit(dynamic_update_index_in_dim)/dynamic_update_slice | solution.py:99
  57.8 1.3 dynamic_slice.129
  60.7 1.3 compare_convert_fusion.4
  66.0 1.6 fusion.151
  67.6 1.8 fusion.152
  70.7 11.3 %dynamic_update_slice.6 = f32[8,256,7,64]{1,0,3,2:T(8,128)} dynamic-update-slice(f32[8,256,7,64]{1,0,3,2:T(8,128)} %get-tuple-element.315, f32[1,256,7,64]{1,0,3,2:T(1,128)} %copy.140, s32[]{:T(128)} %get-tuple-element.313, s32[]{:T(128)} %constant.69.clone.1..sunk, s32[]{:T(128)} %constant.69.clone.1..sunk, s32[]{:T(128)} %constant.69.clone.1..sunk) | dynamic-update-slice | bytes 917508 | tf_op jit(solution)/shard_map/while/body/jit(dynamic_update_index_in_dim)/dynamic_update_slice | solution.py:99
  85.0 1.3 dynamic_slice.129
  87.8 1.3 compare_convert_fusion.4
  93.1 1.6 fusion.151
  94.7 1.8 fusion.152
  97.8 11.3 %dynamic_update_slice.6 = f32[8,256,7,64]{1,0,3,2:T(8,128)} dynamic-update-slice(f32[8,256,7,64]{1,0,3,2:T(8,128)} %get-tuple-element.315, f32[1,256,7,64]{1,0,3,2:T(1,128)} %copy.140, s32[]{:T(128)} %get-tuple-element.313, s32[]{:T(128)} %constant.69.clone.1..sunk, s32[]{:T(128)} %constant.69.clone.1..sunk, s32[]{:T(128)} %constant.69.clone.1..sunk) | dynamic-update-slice | bytes 917508 | tf_op jit(solution)/shard_map/while/body/jit(dynamic_update_index_in_dim)/dynamic_update_slice | solution.py:99
  112.1 1.3 dynamic_slice.129
  115.0 1.3 compare_convert_fusion.4
  120.3 1.6 fusion.151
  121.9 1.8 fusion.152
  125.0 11.3 %dynamic_update_slice.6 = f32[8,256,7,64]{1,0,3,2:T(8,128)} dynamic-update-slice(f32[8,256,7,64]{1,0,3,2:T(8,128)} %get-tuple-element.315, f32[1,256,7,64]{1,0,3,2:T(1,128)} %copy.140, s32[]{:T(128)} %get-tuple-element.313, s32[]{:T(128)} %constant.69.clone.1..sunk, s32[]{:T(128)} %constant.69.clone.1..sunk, s32[]{:T(128)} %constant.69.clone.1..sunk) | dynamic-update-slice | bytes 917508 | tf_op jit(solution)/shard_map/while/body/jit(dynamic_update_index_in_dim)/dynamic_update_slice | solution.py:99
  139.3 1.3 dynamic_slice.129
  142.1 1.3 compare_convert_fusion.4
  147.4 1.6 fusion.151
  149.0 1.8 fusion.152
  152.1 11.3 %dynamic_update_slice.6 = f32[8,256,7,64]{1,0,3,2:T(8,128)} dynamic-update-slice(f32[8,256,7,64]{1,0,3,2:T(8,128)} %get-tuple-element.315, f32[1,256,7,64]{1,0,3,2:T(1,128)} %copy.140, s32[]{:T(128)} %get-tuple-element.313, s32[]{:T(128)} %constant.69.clone.1..sunk, s32[]{:T(128)} %constant.69.clone.1..sunk, s32[]{:T(128)} %constant.69.clone.1..sunk) | dynamic-update-slice | bytes 917508 | tf_op jit(solution)/shard_map/while/body/jit(dynamic_update_index_in_dim)/dynamic_update_slice | solution.py:99
  166.4 1.3 dynamic_slice.129
  169.3 1.3 compare_convert_fusion.4
  174.6 1.6 fusion.151
  176.2 1.8 fusion.152
  179.3 11.3 %dynamic_update_slice.6 = f32[8,256,7,64]{1,0,3,2:T(8,128)} dynamic-update-slice(f32[8,256,7,64]{1,0,3,2:T(8,128)} %get-tuple-element.315, f32[1,256,7,64]{1,0,3,2:T(1,128)} %copy.140, s32[]{:T(128)} %get-tuple-element.313, s32[]{:T(128)} %constant.69.clone.1..sunk, s32[]{:T(128)} %constant.69.clone.1..sunk, s32[]{:T(128)} %constant.69.clone.1..sunk) | dynamic-update-slice | bytes 917508 | tf_op jit(solution)/shard_map/while/body/jit(dynamic_update_index_in_dim)/dynamic_update_slice | solution.py:99
  193.6 1.3 dynamic_slice.129
  196.4 1.3 compare_convert_fusion.4
  201.7 1.6 fusion.151
  203.3 1.8 fusion.152
  206.4 11.3 %dynamic_update_slice.6 = f32[8,256,7,64]{1,0,3,2:T(8,128)} dynamic-update-slice(f32[8,256,7,64]{1,0,3,2:T(8,128)} %get-tuple-element.315, f32[1,256,7,64]{1,0,3,2:T(1,128)} %copy.140, s32[]{:T(128)} %get-tuple-element.313, s32[]{:T(128)} %constant.69.clone.1..sunk, s32[]{:T(128)} %constant.69.clone.1..sunk, s32[]{:T(128)} %constant.69.clone.1..sunk) | dynamic-update-slice | bytes 917508 | tf_op jit(solution)/shard_map/while/body/jit(dynamic_update_index_in_dim)/dynamic_update_slice | solution.py:99
  220.7 1.3 dynamic_slice.129
  223.6 1.3 compare_convert_fusion.4
  228.9 1.6 fusion.151
  230.5 1.8 fusion.152
  233.6 11.3 %dynamic_update_slice.6 = f32[8,256,7,64]{1,0,3,2:T(8,128)} dynamic-update-slice(f32[8,256,7,64]{1,0,3,2:T(8,128)} %get-tuple-element.315, f32[1,256,7,64]{1,0,3,2:T(1,128)} %copy.140, s32[]{:T(128)} %get-tuple-element.313, s32[]{:T(128)} %constant.69.clone.1..sunk, s32[]{:T(128)} %constant.69.clone.1..sunk, s32[]{:T(128)} %constant.69.clone.1..sunk) | dynamic-update-slice | bytes 917508 | tf_op jit(solution)/shard_map/while/body/jit(dynamic_update_index_in_dim)/dynamic_update_slice | solution.py:99
  247.2 1.9 convert_element_type.191
  249.1 1.7 copy.90
  252.5 92.2 %psum.7 = f32[2048,2]{0,1:T(2,128)S(1)} all-reduce(f32[2048,2]{0,1:T(2,128)S(1)} %broadcast_multiply_fusion.1), channel_id=1, replica_groups=mesh['dp'=16,'tensor'=16] {'tensor'}, use_global_device_ids=true, to_apply=%region_5.6 | all-reduce | flops 4096 | bytes 32768 | tf_op jit(solution)/shard_map/psum | solution.py:126
  344.8 3.9 copy.89
  348.7 11.6 %convolution_convert_fusion = bf16[2048,3584]{1,0:T(8,128)(2,1)} fusion(bf16[448,3584]{1,0:T(8,128)(2,1)S(1)} %copy-done, f32[2048,448]{0,1:T(8,128)S(1)} %bitcast.258, f32[448]{0:T(512)S(1)} %copy-done.13, f32[2048]{0:T(1024)S(1)} %add_rsqrt_fusion, bf16[1,2048,448]{1,2,0:T(8,128)(2,1)S(1)} %copy-done.4), kind=kOutput, calls=%fused_computation.84 | convolution fusion | flops 6592266240 | bytes 23406336 | tf_op jit(solution)/shard_map/dot_general | solution.py:132
  364.6 2.1 convolution_add_fusion.3
  366.7 2.7 reshape.350
  369.4 3.4 copy.134
  372.8 3.3 reshape.351
  376.3 2.3 convolution_convert_fusion.1
  378.6 1.5 copy.69
  380.1 6.6 %all-to-all-start = ((bf16[16,7,4096]{2,1,0:T(8,128)(2,1)}), bf16[16,7,4096]{2,1,0:T(8,128)(2,1)}, u32[]{:S(2)}, u32[]{:S(2)}) async-start(bf16[16,7,4096]{2,1,0:T(8,128)(2,1)} %copy.69), calls=%async_computation.1 | async-start | bytes 2097152 | tf_op jit(solution)/shard_map/all_to_all | solution.py:145
  386.7 17.7 %all-to-all-done = bf16[16,7,4096]{2,1,0:T(8,128)(2,1)} async-done(((bf16[16,7,4096]{2,1,0:T(8,128)(2,1)}), bf16[16,7,4096]{2,1,0:T(8,128)(2,1)}, u32[]{:S(2)}, u32[]{:S(2)}) %all-to-all-start) | async-done | bytes 917536 | tf_op jit(solution)/shard_map/all_to_all | solution.py:145
  404.5 3.2 fusion.83
  407.7 142.0 %reduce-scatter.2.cloned.1.call-done = bf16[128,3584]{1,0:T(8,128)(2,1)} async-done(((bf16[2048,3584]{1,0:T(8,128)(2,1)}), bf16[128,3584]{1,0:T(8,128)(2,1)}) %reduce-scatter.2.cloned.1.call-update) | async-done | bytes 917520 | tf_op jit(solution)/shard_map/reduce_scatter | solution.py:131
  (225 shorter events, 80.1 us)
Async XLA Ops:
  7.2 341.5 %copy-start = (bf16[448,3584]{1,0:T(8,128)(2,1)S(1)}, bf16[448,3584]{1,0:T(8,128)(2,1)}, u32[]{:S(2)}) copy-start(bf16[448,3584]{1,0:T(8,128)(2,1)} %param.21) | copy-start | bytes 9633796
  7.2 542.6 %reduce-scatter.2.cloned.1.call-start = ((), (), s32[]{:S(2)}) async-start(), calls=%async_computation.2 | async-start | bytes 15597568 | tf_op jit(solution)/shard_map/reduce_scatter | solution.py:131
  7.8 8.5 %copy-start.14 = (f32[7]{0:T(128)S(1)}, f32[7]{0:T(128)}, u32[]{:S(2)}) copy-start(f32[7]{0:T(128)} %param.18) | copy-start | bytes 88
  7.8 8.5 %copy-start.7 = (f32[1,2048,7]{1,0,2:T(1,128)S(1)}, f32[1,2048,7]{1,0,2:T(1,128)}, u32[]{:S(2)}) copy-start(f32[1,2048,7]{1,0,2:T(1,128)} %param.17) | copy-start | bytes 172036
  18.8 0.6 copy-start.5
  23.3 5.3 copy-start.8
  30.0 3.5 copy-start.10
  36.7 3.7 copy-start.15
  42.3 14.9 %copy-start.11 = (f32[8,7]{1,0:T(8,128)S(1)}, f32[8,7]{1,0:T(8,128)}, u32[]{:S(2)}) copy-start(f32[8,7]{1,0:T(8,128)} %copy-done.10) | copy-start | bytes 676 | tf_op jit(solution)/shard_map/while
  57.1 3.5 copy-start.10
  63.9 3.7 copy-start.15
  69.4 14.9 %copy-start.11 = (f32[8,7]{1,0:T(8,128)S(1)}, f32[8,7]{1,0:T(8,128)}, u32[]{:S(2)}) copy-start(f32[8,7]{1,0:T(8,128)} %copy-done.10) | copy-start | bytes 676 | tf_op jit(solution)/shard_map/while
  84.3 3.5 copy-start.10
  91.0 3.7 copy-start.15
  96.6 14.9 %copy-start.11 = (f32[8,7]{1,0:T(8,128)S(1)}, f32[8,7]{1,0:T(8,128)}, u32[]{:S(2)}) copy-start(f32[8,7]{1,0:T(8,128)} %copy-done.10) | copy-start | bytes 676 | tf_op jit(solution)/shard_map/while
  111.4 3.5 copy-start.10
  118.2 3.7 copy-start.15
  123.7 14.9 %copy-start.11 = (f32[8,7]{1,0:T(8,128)S(1)}, f32[8,7]{1,0:T(8,128)}, u32[]{:S(2)}) copy-start(f32[8,7]{1,0:T(8,128)} %copy-done.10) | copy-start | bytes 676 | tf_op jit(solution)/shard_map/while
  138.6 3.5 copy-start.10
  145.3 3.7 copy-start.15
  150.9 14.9 %copy-start.11 = (f32[8,7]{1,0:T(8,128)S(1)}, f32[8,7]{1,0:T(8,128)}, u32[]{:S(2)}) copy-start(f32[8,7]{1,0:T(8,128)} %copy-done.10) | copy-start | bytes 676 | tf_op jit(solution)/shard_map/while
  165.7 3.5 copy-start.10
  172.5 3.7 copy-start.15
  178.0 14.9 %copy-start.11 = (f32[8,7]{1,0:T(8,128)S(1)}, f32[8,7]{1,0:T(8,128)}, u32[]{:S(2)}) copy-start(f32[8,7]{1,0:T(8,128)} %copy-done.10) | copy-start | bytes 676 | tf_op jit(solution)/shard_map/while
  192.9 3.5 copy-start.10
  199.6 3.7 copy-start.15
  205.2 14.9 %copy-start.11 = (f32[8,7]{1,0:T(8,128)S(1)}, f32[8,7]{1,0:T(8,128)}, u32[]{:S(2)}) copy-start(f32[8,7]{1,0:T(8,128)} %copy-done.10) | copy-start | bytes 676 | tf_op jit(solution)/shard_map/while
  220.0 3.5 copy-start.10
  226.8 3.7 copy-start.15
  232.3 14.9 %copy-start.11 = (f32[8,7]{1,0:T(8,128)S(1)}, f32[8,7]{1,0:T(8,128)}, u32[]{:S(2)}) copy-start(f32[8,7]{1,0:T(8,128)} %copy-done.10) | copy-start | bytes 676 | tf_op jit(solution)/shard_map/while
  249.1 2.0 copy-start.1
  251.2 1.3 copy-start.12
  344.8 3.9 copy-start.4
  344.8 3.9 copy-start.13
  360.4 0.8 copy-start.6
  360.4 2.1 copy-start.3
  360.4 2.3 copy-start.2
  372.8 3.3 copy-start.9
  380.1 24.4 %all-to-all-start = ((bf16[16,7,4096]{2,1,0:T(8,128)(2,1)}), bf16[16,7,4096]{2,1,0:T(8,128)(2,1)}, u32[]{:S(2)}, u32[]{:S(2)}) async-start(bf16[16,7,4096]{2,1,0:T(8,128)(2,1)} %copy.69), calls=%async_computation.1 | async-start | bytes 2097152 | tf_op jit(solution)/shard_map/all_to_all | solution.py:145
Sparse Core Ops, SparseCore 0:
  360.5 189.1 reduce-scatter.1
where the time goes:
time: 562 us; the launch traced here: 557 us
  waiting for transfers between devices  160 us (28%)
  local copies, waits for them, and re-layouts  158 us (28%)
  blocking collectives  92.2 us (16%)
  matrix products  90.4 us (16%)
  other arithmetic  23.5 us (4%)
  between operations  14.3 us (3%)
  loops' own time  11.8 us (2%)
  starting transfers between devices  6.61 us (1%)
    reduce_scatter x1, waiting for transfers between devices, local(): lax.psum_scatter(jnp.dot(rounded, out_weight, preferred_element_type=jnp....  142 us
    dynamic_update_slice x16, local copies, waits for them, and re-layouts, local(): lax.scan(advance, jnp.zeros((dev_heads, HEAD, STATE), jnp.float32), block...  100 us
    psum x1, blocking collectives, local(): group_stat = lax.psum(sum_sq[:, None] * group_hot[None, :], 'tensor')  92.2 us
    dot_general x25, matrix products, split_einsum(): jnp.einsum(form, lower, narrow, preferred_element_type=jnp.float32)  33.6 us
    dot_general x25, matrix products, split_einsum(): first = jnp.einsum(form, upper, narrow, preferred_element_type=jnp.float32)  30.6 us
    all_to_all x1, waiting for transfers between devices, local(): lax.all_to_all(outbound.astype(jnp.bfloat16), 'dp', split_axis=0, concat_...  17.7 us
    unnamed x39, local copies, waits for them, and re-layouts  17.2 us
    dynamic_slice x24, local copies, waits for them, and re-layouts, local(): lax.scan(advance, jnp.zeros((dev_heads, HEAD, STATE), jnp.float32), block...  16.8 us
  transfers between devices with their start and end apart: 2, of which 2 were waited for; matrix products, arithmetic and copies ran while one was open for 4% of the time, Pallas kernels for 0%

commit v1 on v0

--- a/solution.py
+++ b/solution.py
@@ -51,52 +51,45 @@
     cum_log = jnp.cumsum(-decay_rate[None, :] * step_size, axis=0)
     seg_row = segment[0]
     block_count = stream_len // BLOCK
-    prev_cum = jnp.concatenate([jnp.zeros((1, dev_heads), jnp.float32), cum_log[:-1]], axis=0)[
-        ::BLOCK
-    ]
-    prev_seg = jnp.concatenate([jnp.full((1,), -1, seg_row.dtype), seg_row[:-1]], axis=0)[::BLOCK]
-    block_inputs = (
-        inner_x[0].reshape(block_count, BLOCK, dev_heads, HEAD),
-        cum_log.reshape(block_count, BLOCK, dev_heads),
-        step_size.reshape(block_count, BLOCK, dev_heads),
-        seg_row.reshape(block_count, BLOCK),
-        b_cols.reshape(block_count, BLOCK, STATE),
-        c_cols.reshape(block_count, BLOCK, STATE),
-        prev_cum,
-        prev_seg,
+    x_blk = inner_x[0].reshape(block_count, BLOCK, dev_heads, HEAD)
+    cum_blk = cum_log.reshape(block_count, BLOCK, dev_heads)
+    step_blk = step_size.reshape(block_count, BLOCK, dev_heads)
+    seg_blk = seg_row.reshape(block_count, BLOCK)
+    b_blk = b_cols.reshape(block_count, BLOCK, STATE)
+    c_blk = c_cols.reshape(block_count, BLOCK, STATE)
+    positions = jnp.arange(BLOCK)
+    scores = jnp.einsum("btn,bsn->bts", c_blk, b_blk, preferred_element_type=jnp.float32)
+    causal_mask = (positions[None, None, :] <= positions[None, :, None]) & (
+        seg_blk[:, :, None] == seg_blk[:, None, :]
     )
-    positions = jnp.arange(BLOCK)
-
-    def advance(carried, block_in):
-        x_blk, cum_blk, step_blk, seg_blk, b_blk, c_blk, prev_c, prev_s = block_in
-        scores = jnp.dot(c_blk, b_blk.T, preferred_element_type=jnp.float32)
-        causal_mask = (positions[None, :] <= positions[:, None]) & (
-            seg_blk[:, None] == seg_blk[None, :]
-        )
-        log_gap = cum_blk.T[:, :, None] - cum_blk.T[:, None, :]
-        weights = (
-            jnp.exp(jnp.where(causal_mask[None], log_gap, -jnp.inf))
-            * step_blk.T[:, None, :]
-            * scores[None]
-        )
-        intra_part = split_einsum("hts,shp->thp", weights, x_blk)
-        live_rows = (seg_blk == prev_s).astype(jnp.float32)
-        carry_decay = jnp.exp(cum_blk - prev_c[None, :]) * live_rows[:, None]
-        carry_part = split_einsum("hpn,tn->thp", carried, c_blk) * carry_decay[:, :, None]
-        outputs = intra_part + carry_part + skip_gain[None, :, None] * x_blk.astype(jnp.float32)
-        last_seg = seg_blk[-1]
-        last_cum = cum_blk[-1]
-        keep_rows = (last_seg == prev_s).astype(jnp.float32)
-        pull_back = (
-            jnp.exp(last_cum[None, :] - cum_blk)
-            * step_blk
-            * (seg_blk == last_seg).astype(jnp.float32)[:, None]
-        )
-        added_part = split_einsum("shp,sn->hpn", pull_back[:, :, None] * x_blk, b_blk)
-        carried = carried * (jnp.exp(last_cum - prev_c) * keep_rows)[:, None, None] + added_part
-        return (carried, outputs)
-
-    _, outputs = lax.scan(advance, jnp.zeros((dev_heads, HEAD, STATE), jnp.float32), block_inputs)
+    cum_t = cum_blk.transpose(0, 2, 1)
+    log_gap = cum_t[:, :, :, None] - cum_t[:, :, None, :]
+    weights = (
+        jnp.exp(jnp.where(causal_mask[:, None], log_gap, -jnp.inf))
+        * step_blk.transpose(0, 2, 1)[:, :, None, :]
+        * scores[:, None]
+    )
+    intra_part = split_einsum("bhts,bshp->bthp", weights, x_blk)
+    last_seg = seg_blk[:, -1]
+    last_cum = cum_blk[:, -1]
+    pull_back = (
+        jnp.exp(last_cum[:, None, :] - cum_blk)
+        * step_blk
+        * (seg_blk == last_seg[:, None]).astype(jnp.float32)[:, :, None]
+    )
+    added = split_einsum("bshp,bsn->bhpn", pull_back[:, :, :, None] * x_blk, b_blk)
+    prev_cum = jnp.concatenate([jnp.zeros((1, dev_heads), jnp.float32), last_cum[:-1]], axis=0)
+    prev_seg = jnp.concatenate([jnp.full((1,), -1, seg_row.dtype), last_seg[:-1]], axis=0)
+    blocks = jnp.arange(block_count)
+    earlier = blocks[None, :] < blocks[:, None]
+    mix_ok = earlier & (last_seg[None, :] == prev_seg[:, None])
+    mix_gap = prev_cum[:, None, :] - last_cum[None, :, :]
+    mix = jnp.exp(jnp.where(mix_ok[:, :, None], mix_gap, -jnp.inf))
+    carried = jnp.sum(mix[:, :, :, None, None] * added[None], axis=1)
+    live_rows = (seg_blk == prev_seg[:, None]).astype(jnp.float32)
+    carry_decay = jnp.exp(cum_blk - prev_cum[:, None, :]) * live_rows[:, :, None]
+    carry_part = split_einsum("bhpn,btn->bthp", carried, c_blk) * carry_decay[:, :, :, None]
+    outputs = intra_part + carry_part + skip_gain[None, None, :, None] * x_blk.astype(jnp.float32)
     mixer_y = outputs.reshape(stream_len, dev_width)
     members = (seg_row[None, :] == jnp.arange(REQS)[:, None]).astype(jnp.float32)
     end_index = (

time: 562 us -> 361 us (0.64)
  local copies, waits for them, and re-layouts: 158 us -> 30.9 us
  matrix products: 90.4 us -> 43.2 us
  loops' own time: 11.8 us -> 0 us
  other arithmetic: 23.5 us -> 13.5 us
    dynamic_update_slice x16 -> x0, local copies, waits for them, and re-layouts: 100 us -> none  [local(): lax.scan(advance, jnp.zeros((dev_heads, HEAD, STATE), jnp.float32), block...]
    dot_general x25 -> x4, matrix products: 30.6 us -> 7.99 us  [split_einsum(): first = jnp.einsum(form, upper, narrow, preferred_element_type=jnp.float32)]
    dot_general x25 -> x4, matrix products: 33.6 us -> 11.7 us  [split_einsum(): jnp.einsum(form, lower, narrow, preferred_element_type=jnp.float32)]
    dynamic_slice x25 -> x1, local copies, waits for them, and re-layouts: 19.7 us -> 2.52 us  [local(): b_cols = lax.dynamic_slice_in_dim(input_b[0], group_idx * STATE, STATE, 1)]
    another operation x1 -> x0, loops' own time: 11.8 us -> none  [local(): lax.scan(advance, jnp.zeros((dev_heads, HEAD, STATE), jnp.float32), block...]
    convert_element_type x8 -> x1, other arithmetic: 10.7 us -> 0.67 us  [local(): live_rows = (seg_blk == prev_seg[:, None]).astype(jnp.float32)]
    slice x19 -> x5, local copies, waits for them, and re-layouts: 8.63 us -> 0.46 us  [the longest x8 5.34 us: advance(): last_seg = seg_blk[-1]]
    dot_general x8 -> x1, matrix products: 7.86 us -> 1.45 us  [local(): jnp.einsum('btn,bsn->bts', c_blk, b_blk, preferred_element_type=jnp.float32)]
  transfers between devices with their start and end apart: 2 -> 2, of which waited for: 2 -> 2; matrix products, arithmetic and copies ran while one was open for 4% -> 6% of each run, Pallas kernels for 0% -> 0%
where the time goes in v1:
time: 361 us
  waiting for transfers between devices  160 us (44%)
  blocking collectives  92.2 us (26%)
  matrix products  43.2 us (12%)
  local copies, waits for them, and re-layouts  30.9 us (9%)
  between operations  14.4 us (4%)
  other arithmetic  13.5 us (4%)
  starting transfers between devices  6.55 us (2%)
    reduce_scatter x1, waiting for transfers between devices, local(): lax.psum_scatter(jnp.dot(rounded, out_weight, preferred_element_type=jnp....  142 us
    psum x1, blocking collectives, local(): group_stat = lax.psum(sum_sq[:, None] * group_hot[None, :], 'tensor')  92.2 us
    all_to_all x1, waiting for transfers between devices, local(): lax.all_to_all(outbound.astype(jnp.bfloat16), 'dp', split_axis=0, concat_...  17.8 us
    dot_general x1, matrix products, local(): jnp.dot(rounded, out_weight, preferred_element_type=jnp.float32)  15.2 us
    unnamed x49, local copies, waits for them, and re-layouts  13 us
    dot_general x4, matrix products, split_einsum(): jnp.einsum(form, lower, narrow, preferred_element_type=jnp.float32)  11.7 us
    dot_general x4, matrix products, split_einsum(): first = jnp.einsum(form, upper, narrow, preferred_element_type=jnp.float32)  7.99 us
  transfers between devices with their start and end apart: 2, of which 2 were waited for; matrix products, arithmetic and copies ran while one was open for 6% of the time, Pallas kernels for 0%

profile of v1, /device:TPU:32, one launch (start us, length us, event | category | flops | bytes accessed | tf_op | source)
XLA Modules:
  0.0 360.7 jit_solution(5995153483289453547)
XLA Ops:
  7.2 0.5 broadcast.229
  7.8 1.4 reduce.9
  9.2 0.1 slice.36
  9.3 0.7 neg.22
  10.0 0.9 multiply_bitcast_fusion
  10.9 2.0 reduce-window.6
  12.9 0.2 slice_reduce_fusion
  13.1 0.2 reduce-window.9
  13.2 0.1 add_bitcast_fusion
  13.3 0.6 copy-done.5
  14.0 0.1 slice.37
  14.1 0.1 slice.38
  14.1 0.1 copy.169
  14.2 0.1 copy.168
  14.3 0.9 dynamic-slice_reduce_fusion
  15.2 0.6 and_select_fusion
  15.8 0.7 compare_convert_fusion
  16.5 0.7 fusion.58
  17.1 0.6 copy.241
  17.8 0.6 iota_compare_fusion
  18.4 3.3 copy.177
  21.8 0.1 copy.170
  21.9 0.8 reduce.3
  22.7 0.1 copy.171
  22.8 2.5 constant_dynamic-slice_fusion
  25.3 1.2 copy.167
  26.7 1.0 copy.120
  27.6 1.3 compare_and_fusion
  28.9 1.5 fusion.46
  30.4 0.1 exponential_multiply_fusion
  30.5 5.6 %fusion.4 = f32[8,7,256,64]{2,3,1,0:T(8,128)S(1)} fusion(f32[8,256,256]{2,1,0:T(8,128)S(1)} %fusion.46, f32[8,7,256]{2,1,0:T(8,128)S(1)} %get-tuple-element.6, f32[8,7,256]{2,1,0:T(8,128)S(1)} %copy.120, pred[8,256,256]{2,1,0:T(8,128)(4,1)S(1)} %compare_and_fusion, bf16[8,256,7,64]{1,0,3,2:T(8,128)(2,1)S(1)} %bitcast.162), kind=kOutput, calls=%fused_computation.7 | convolution fusion | flops 488112128 | bytes 8241152 | tf_op jit(solution)/shard_map/bhts,bshp->bthp/dot_general | solution.py:26
  36.1 6.2 %fusion.1 = f32[8,7,256,64]{2,3,1,0:T(8,128)S(1)} fusion(f32[8,256,256]{2,1,0:T(8,128)S(1)} %fusion.46, f32[8,7,256]{2,1,0:T(8,128)S(1)} %get-tuple-element.6, f32[8,7,256]{2,1,0:T(8,128)S(1)} %copy.120, pred[8,256,256]{2,1,0:T(8,128)(4,1)S(1)} %compare_and_fusion, bf16[8,256,7,64]{1,0,3,2:T(8,128)(2,1)S(1)} %bitcast.163), kind=kOutput, calls=%fused_computation.5 | convolution fusion | flops 499122176 | bytes 8241152 | tf_op jit(solution)/shard_map/bhts,bshp->bthp/dot_general | solution.py:27
  42.3 0.4 convert_element_type.188
  42.8 1.7 copy.179
  44.5 0.7 fusion.23
  45.2 0.6 fusion.32
  45.8 0.1 select_exponential_fusion
  45.9 1.8 multiply_reduce_fusion
  47.7 0.6 fusion.44
  48.3 2.8 multiply_reduce_fusion.1
  51.1 2.1 copy.144
  53.2 3.7 %copy.178 = f32[56,8,8,256]{3,1,2,0:T(8,128)} copy(f32[56,8,8,256]{3,2,1,0:T(8,128)S(1)} %bitcast.160) | data formatting | bytes 7340032
  56.9 0.1 broadcast_multiply_fusion.1
  57.0 92.2 %psum.7 = f32[2048,2]{0,1:T(2,128)S(1)} all-reduce(f32[2048,2]{0,1:T(2,128)S(1)} %broadcast_multiply_fusion.1), channel_id=1, replica_groups=mesh['dp'=16,'tensor'=16] {'tensor'}, use_global_device_ids=true, to_apply=%region_4.5 | all-reduce | flops 4096 | bytes 32768 | tf_op jit(solution)/shard_map/psum | solution.py:119
  149.2 0.1 multiply_reduce_fusion.2
  149.3 15.2 %convolution_convert_fusion = bf16[2048,3584]{1,0:T(8,128)(2,1)} fusion(bf16[448,3584]{1,0:T(8,128)(2,1)S(1)} %copy-done, f32[2048,448]{0,1:T(8,128)} %bitcast.174, f32[448]{0:T(512)S(1)} %copy-done.15, f32[2048]{0:T(1024)S(1)} %add_rsqrt_fusion, bf16[1,2048,448]{1,2,0:T(8,128)(2,1)} %param.12), kind=kOutput, calls=%fused_computation | convolution fusion | flops 6592266240 | bytes 23406336 | tf_op jit(solution)/shard_map/dot_general | solution.py:125
  164.5 0.7 copy-done.9
  165.2 0.1 convert_reduce_fusion
  165.3 0.2 fusion.54
  165.5 1.1 fusion.21
  166.6 0.2 broadcast_multiply_fusion
  166.8 0.7 fusion.12
  167.6 1.1 fusion.66
  168.7 2.1 convolution_add_fusion
  170.8 2.7 reshape.333
  173.5 3.4 copy.237
  176.9 3.3 reshape.334
  180.2 2.3 convolution_convert_fusion.1
  182.6 1.5 copy.148
  184.1 6.5 %all-to-all-start = ((bf16[16,7,4096]{2,1,0:T(8,128)(2,1)}), bf16[16,7,4096]{2,1,0:T(8,128)(2,1)}, u32[]{:S(2)}, u32[]{:S(2)}) async-start(bf16[16,7,4096]{2,1,0:T(8,128)(2,1)} %copy.148), calls=%async_computation.1 | async-start | bytes 2097152 | tf_op jit(solution)/shard_map/all_to_all | solution.py:138
  190.6 0.1 compare_reduce_fusion
  190.7 17.8 %all-to-all-done = bf16[16,7,4096]{2,1,0:T(8,128)(2,1)} async-done(((bf16[16,7,4096]{2,1,0:T(8,128)(2,1)}), bf16[16,7,4096]{2,1,0:T(8,128)(2,1)}, u32[]{:S(2)}, u32[]{:S(2)}) %all-to-all-start) | async-done | bytes 917536 | tf_op jit(solution)/shard_map/all_to_all | solution.py:138
  208.5 3.2 fusion.39
  211.7 142.2 %reduce-scatter.2.cloned.1.call-done = bf16[128,3584]{1,0:T(8,128)(2,1)} async-done(((bf16[2048,3584]{1,0:T(8,128)(2,1)}), bf16[128,3584]{1,0:T(8,128)(2,1)}) %reduce-scatter.2.cloned.1.call-update) | async-done | bytes 917520 | tf_op jit(solution)/shard_map/reduce_scatter | solution.py:124
  (47 shorter events, 0.4 us)
Async XLA Ops:
  7.2 142.1 %copy-start = (bf16[448,3584]{1,0:T(8,128)(2,1)S(1)}, bf16[448,3584]{1,0:T(8,128)(2,1)}, u32[]{:S(2)}) copy-start(bf16[448,3584]{1,0:T(8,128)(2,1)} %param.19) | copy-start | bytes 9633796
  7.2 14.7 %copy-start.8 = (f32[1,2048,7]{1,0,2:T(1,128)S(1)}, f32[1,2048,7]{1,0,2:T(1,128)}, u32[]{:S(2)}) copy-start(f32[1,2048,7]{1,0,2:T(1,128)} %param.15) | copy-start | bytes 172036
  7.2 346.7 %reduce-scatter.2.cloned.1.call-start = ((), (), s32[]{:S(2)}) async-start(), calls=%async_computation.2 | async-start | bytes 15597568 | tf_op jit(solution)/shard_map/reduce_scatter | solution.py:124
  13.3 0.6 copy-start.5
  26.6 3.8 %copy-start.7 = (f32[2048,7]{0,1:T(8,128)S(1)}, f32[2048,7]{0,1:T(8,128)}, u32[]{:S(2)}) copy-start(f32[2048,7]{0,1:T(8,128)} %reduce.3) | copy-start | bytes 172036
  26.6 3.8 %copy-start.10 = (f32[8,256]{1,0:T(8,128)S(1)}, f32[8,256]{1,0:T(8,128)}, u32[]{:S(2)}) copy-start(f32[8,256]{1,0:T(8,128)} %get-tuple-element.7) | copy-start | bytes 24580
  26.6 3.8 %copy-start.11 = (f32[8,256]{1,0:T(8,128)S(1)}, f32[8,256]{1,0:T(8,128)}, u32[]{:S(2)}) copy-start(f32[8,256]{1,0:T(8,128)} %get-tuple-element.8) | copy-start | bytes 24580
  26.6 3.9 %copy-start.1 = (bf16[56,8,8,256]{3,2,1,0:T(8,128)(2,1)S(1)}, bf16[56,8,8,256]{3,2,1,0:T(8,128)(2,1)}, u32[]{:S(2)}) copy-start(bf16[56,8,8,256]{3,2,1,0:T(8,128)(2,1)} %copy.177) | copy-start | bytes 5505028
  36.1 6.2 %copy-start.4 = (bf16[1,2048,448]{1,2,0:T(8,128)(2,1)S(1)}, bf16[1,2048,448]{1,2,0:T(8,128)(2,1)}, u32[]{:S(2)}) copy-start(bf16[1,2048,448]{1,2,0:T(8,128)(2,1)} %param.12) | copy-start | bytes 5505028
  45.1 0.7 copy-start.13
  45.1 2.5 copy-start.3
  47.7 0.7 copy-start.16
  53.2 96.1 %copy-start.15 = (f32[448]{0:T(512)S(1)}, f32[448]{0:T(512)}, u32[]{:S(2)}) copy-start(f32[448]{0:T(512)} %param.18) | copy-start | bytes 5380
  164.5 0.7 copy-start.9
  164.5 0.8 copy-start.6
  164.5 2.3 copy-start.2
  173.5 6.7 %copy-start.14 = (s32[8]{0:T(128)S(1)}, s32[8]{0:T(128)}, u32[]{:S(2)}) copy-start(s32[8]{0:T(128)} %get-tuple-element.11) | copy-start | bytes 100
  176.9 13.7 %copy-start.12 = (s32[16,8]{0,1:T(8,128)S(1)}, s32[16,8]{0,1:T(8,128)}, u32[]{:S(2)}) copy-start(s32[16,8]{0,1:T(8,128)} %param.21) | copy-start | bytes 1540
  184.1 24.4 %all-to-all-start = ((bf16[16,7,4096]{2,1,0:T(8,128)(2,1)}), bf16[16,7,4096]{2,1,0:T(8,128)(2,1)}, u32[]{:S(2)}, u32[]{:S(2)}) async-start(bf16[16,7,4096]{2,1,0:T(8,128)(2,1)} %copy.148), calls=%async_computation.1 | async-start | bytes 2097152 | tf_op jit(solution)/shard_map/all_to_all | solution.py:138
Sparse Core Ops, SparseCore 0:
  164.6 189.2 reduce-scatter.1

commit v2 on v1

--- a/solution.py
+++ b/solution.py
@@ -1,7 +1,7 @@
 import jax
 import jax.numpy as jnp
 from jax import lax
-from jax.sharding import PartitionSpec as P
+from jax.sharding import Mesh, PartitionSpec as P
 
 HEADS = 112
 HEAD = 64
@@ -13,6 +13,8 @@
 
 
 HIGHEST = lax.Precision.HIGHEST
+TENSOR = ("head_group", "y_rest", "z_hi", "core")
+GROUP_MATES = TENSOR[1:]
 
 
 def split_pair(values):
@@ -43,7 +45,7 @@
     stream_len = inner_x.shape[1]
     dev_width = inner_x.shape[2]
     dev_heads = decay_rate.shape[0]
-    tensor_idx = lax.axis_index("tensor")
+    tensor_idx = lax.axis_index(TENSOR)
     group_idx = tensor_idx * dev_heads // (HEADS // NGROUPS)
     b_cols = lax.dynamic_slice_in_dim(input_b[0], group_idx * STATE, STATE, 1)
     c_cols = lax.dynamic_slice_in_dim(output_c[0], group_idx * STATE, STATE, 1)
@@ -115,15 +117,14 @@
     )
     gated = mixer_y * jax.nn.silu(gate_z[0].astype(jnp.float32))
     sum_sq = jnp.sum(gated * gated, axis=1)
-    group_hot = (jnp.arange(NGROUPS) == group_idx).astype(jnp.float32)
-    group_stat = lax.psum(sum_sq[:, None] * group_hot[None, :], "tensor")
-    mean_sq = jnp.sum(group_stat * group_hot[None, :], axis=1) / (INNER // NGROUPS)
+    group_stat = lax.all_gather(sum_sq, GROUP_MATES, tiled=True)
+    mean_sq = jnp.sum(group_stat.reshape(-1, stream_len), axis=0) / (INNER // NGROUPS)
     rounded = (gated * lax.rsqrt(mean_sq + 1e-05)[:, None] * norm_gain[None, :]).astype(
         jnp.bfloat16
     )
     projected = lax.psum_scatter(
         jnp.dot(rounded, out_weight, preferred_element_type=jnp.float32).astype(jnp.bfloat16),
-        "tensor",
+        TENSOR,
         scatter_dimension=0,
         tiled=True,
     )
@@ -147,18 +148,25 @@
 
 
 def solution(mesh):
+    dp_size, tensor_size = mesh.devices.shape
+    groups = NGROUPS
+    rest = tensor_size // (2 * 2 * groups)
+    split = Mesh(
+        mesh.devices.reshape(dp_size, groups, rest, 2, 2), ("dp",) + TENSOR
+    )
+    tp = TENSOR
     in_specs = (
-        P("dp", None, "tensor"),
-        P("dp", None, "tensor"),
+        P("dp", None, tp),
+        P("dp", None, tp),
         P("dp", None, None),
         P("dp", None, None),
-        P("dp", None, "tensor"),
-        P("tensor"),
-        P("tensor"),
-        P("tensor"),
-        P("tensor", None),
+        P("dp", None, tp),
+        P(tp),
+        P(tp),
+        P(tp),
+        P(tp, None),
         P("dp", None),
         P(),
     )
-    out_specs = (P("dp", "tensor", None), P("dp", "tensor", None))
-    return jax.shard_map(local, mesh=mesh, in_specs=in_specs, out_specs=out_specs, check_vma=False)
+    out_specs = (P("dp", tp, None), P("dp", tp, None))
+    return jax.shard_map(local, mesh=split, in_specs=in_specs, out_specs=out_specs, check_vma=False)

time: 361 us -> 288 us (0.80)
  blocking collectives: 92.2 us -> 21.5 us
  waiting for transfers between devices: 160 us -> 156 us
    psum x1 -> x0, blocking collectives: 92.2 us -> none  [local(): group_stat = lax.psum(sum_sq[:, None] * group_hot[None, :], 'tensor')]
    reduce_scatter x1, waiting for transfers between devices: 142 us -> 99.6 us  [local(): lax.psum_scatter(jnp.dot(rounded, out_weight, preferred_element_type=jnp....]
    all_to_all x1, waiting for transfers between devices: 17.8 us -> 56 us  [local(): lax.all_to_all(outbound.astype(jnp.bfloat16), 'dp', split_axis=0, concat_...]
    all_gather x0 -> x1, blocking collectives: none -> 21.5 us  [local(): group_stat = lax.all_gather(sum_sq, GROUP_MATES, tiled=True)]
  transfers between devices with their start and end apart: 2 -> 2, of which waited for: 2 -> 2; matrix products, arithmetic and copies ran while one was open for 6% -> 8% of each run, Pallas kernels for 0% -> 0%
where the time goes in v2:
time: 288 us
  waiting for transfers between devices  156 us (54%)
  matrix products  43.2 us (15%)
  local copies, waits for them, and re-layouts  31.4 us (11%)
  blocking collectives  21.5 us (7%)
  between operations  14.4 us (5%)
  other arithmetic  13.4 us (5%)
  starting transfers between devices  8.28 us (3%)
    reduce_scatter x1, waiting for transfers between devices, local(): lax.psum_scatter(jnp.dot(rounded, out_weight, preferred_element_type=jnp....  99.6 us
    all_to_all x1, waiting for transfers between devices, local(): lax.all_to_all(outbound.astype(jnp.bfloat16), 'dp', split_axis=0, concat_...  56 us
    all_gather x1, blocking collectives, local(): group_stat = lax.all_gather(sum_sq, GROUP_MATES, tiled=True)  21.5 us
    dot_general x1, matrix products, local(): jnp.dot(rounded, out_weight, preferred_element_type=jnp.float32)  15.1 us
    unnamed x49, local copies, waits for them, and re-layouts  13 us
    dot_general x4, matrix products, split_einsum(): jnp.einsum(form, lower, narrow, preferred_element_type=jnp.float32)  11.7 us
    all_to_all x1, starting transfers between devices, local(): lax.all_to_all(outbound.astype(jnp.bfloat16), 'dp', split_axis=0, concat_...  8.25 us
    dot_general x4, matrix products, split_einsum(): first = jnp.einsum(form, upper, narrow, preferred_element_type=jnp.float32)  7.99 us
  transfers between devices with their start and end apart: 2, of which 2 were waited for; matrix products, arithmetic and copies ran while one was open for 8% of the time, Pallas kernels for 0%

profile of v2, /device:TPU:32, one launch (start us, length us, event | category | flops | bytes accessed | tf_op | source)
XLA Modules:
  0.0 287.7 jit_solution(2523831067027346326)
XLA Ops:
  7.2 0.5 broadcast.225
  7.8 1.4 reduce.9
  9.2 0.1 slice.36
  9.3 0.1 slice.35
  9.3 0.7 neg.22
  10.0 0.9 multiply_bitcast_fusion
  10.9 2.0 reduce-window.6
  12.9 0.2 slice_reduce_fusion
  13.1 0.2 reduce-window.9
  13.2 0.1 add_bitcast_fusion
  13.3 0.6 copy-done.5
  14.0 0.1 slice.37
  14.1 0.1 slice.38
  14.1 0.1 copy.169
  14.2 0.1 copy.168
  14.3 0.9 dynamic-slice_reduce_fusion
  15.2 0.6 and_select_fusion
  15.8 0.7 compare_convert_fusion
  16.5 0.7 fusion.58
  17.1 0.6 copy.241
  17.8 0.6 iota_compare_fusion
  18.4 3.3 %copy.177 = bf16[56,8,8,256]{3,2,1,0:T(8,128)(2,1)} copy(bf16[56,8,8,256]{3,1,2,0:T(8,128)(2,1)} %bitcast.168) | data formatting | bytes 3670016
  21.8 0.1 copy.170
  21.9 0.8 reduce.3
  22.7 0.1 copy.171
  22.8 2.5 constant_dynamic-slice_fusion
  25.3 1.2 copy.167
  26.7 1.0 copy.120
  27.6 1.3 compare_and_fusion
  28.9 1.5 fusion.46
  30.4 0.1 exponential_multiply_fusion
  30.5 5.6 %fusion.4 = f32[8,7,256,64]{2,3,1,0:T(8,128)S(1)} fusion(f32[8,256,256]{2,1,0:T(8,128)S(1)} %fusion.46, f32[8,7,256]{2,1,0:T(8,128)S(1)} %get-tuple-element.6, f32[8,7,256]{2,1,0:T(8,128)S(1)} %copy.120, pred[8,256,256]{2,1,0:T(8,128)(4,1)S(1)} %compare_and_fusion, bf16[8,256,7,64]{1,0,3,2:T(8,128)(2,1)S(1)} %bitcast.162), kind=kOutput, calls=%fused_computation.7 | convolution fusion | flops 488112128 | bytes 8241152 | tf_op jit(solution)/shard_map/bhts,bshp->bthp/dot_general | solution.py:28
  36.1 6.2 %fusion.1 = f32[8,7,256,64]{2,3,1,0:T(8,128)S(1)} fusion(f32[8,256,256]{2,1,0:T(8,128)S(1)} %fusion.46, f32[8,7,256]{2,1,0:T(8,128)S(1)} %get-tuple-element.6, f32[8,7,256]{2,1,0:T(8,128)S(1)} %copy.120, pred[8,256,256]{2,1,0:T(8,128)(4,1)S(1)} %compare_and_fusion, bf16[8,256,7,64]{1,0,3,2:T(8,128)(2,1)S(1)} %bitcast.163), kind=kOutput, calls=%fused_computation.5 | convolution fusion | flops 499122176 | bytes 8241152 | tf_op jit(solution)/shard_map/bhts,bshp->bthp/dot_general | solution.py:29
  42.3 0.4 convert_element_type.180
  42.8 1.7 copy.179
  44.5 0.7 fusion.23
  45.1 0.6 fusion.32
  45.8 0.1 select_exponential_fusion
  45.9 1.8 multiply_reduce_fusion
  47.7 0.6 fusion.44
  48.3 2.8 multiply_reduce_fusion.1
  51.1 2.1 copy.144
  53.2 3.7 %copy.178 = f32[56,8,8,256]{3,1,2,0:T(8,128)} copy(f32[56,8,8,256]{3,2,1,0:T(8,128)S(1)} %bitcast.160) | data formatting | bytes 7340032
  56.9 21.5 %all_gather.3 = f32[16384]{0:T(1024)} all-gather(f32[2048]{0:T(1024)S(1)} %bitcast.198), channel_id=1, replica_groups=mesh['dp'=16,'head_group'=2,'y_rest'=2,'z_hi'=2,'core'=2] {'y_rest','z_h..., dimensions={0}, use_global_device_ids=true | all-gather | bytes 73728 | tf_op jit(solution)/shard_map/all_gather | solution.py:120
  78.4 0.9 reshape.329
  79.3 15.1 %convolution_convert_fusion = bf16[2048,3584]{1,0:T(8,128)(2,1)} fusion(bf16[448,3584]{1,0:T(8,128)(2,1)S(1)} %copy-done, f32[2048,448]{0,1:T(8,128)} %bitcast.174, f32[448]{0:T(512)S(1)} %copy-done.15, f32[2048]{0:T(1024)S(1)} %add_rsqrt_fusion, bf16[1,2048,448]{1,2,0:T(8,128)(2,1)} %param.12), kind=kOutput, calls=%fused_computation | convolution fusion | flops 6592266240 | bytes 23406336 | tf_op jit(solution)/shard_map/dot_general | solution.py:126
  94.5 0.7 copy-done.9
  95.2 0.1 convert_reduce_fusion
  95.3 0.2 fusion.54
  95.5 1.1 fusion.21
  96.6 0.2 broadcast_multiply_fusion
  96.8 0.7 fusion.12
  97.6 1.1 fusion.66
  98.7 2.1 convolution_add_fusion
  100.8 2.6 reshape.330
  103.4 3.1 %copy.237 = f32[7,64,8,64]{3,1,0,2:T(8,128)} copy(f32[7,64,8,64]{3,2,1,0:T(8,128)} %reshape.330) | data formatting | bytes 1835008 | tf_op jit(solution)/shard_map/reshape | solution.py:114
  106.5 3.4 %reshape.331 = f32[8,28672]{1,0:T(8,128)} reshape(f32[8,7,64,64]{3,2,1,0:T(8,128)} %bitcast.167) | data formatting | bytes 1835008 | tf_op jit(solution)/shard_map/reshape | solution.py:116
  109.9 2.3 convolution_convert_fusion.1
  112.2 1.5 copy.148
  113.7 8.2 %all-to-all-start = ((bf16[16,7,4096]{2,1,0:T(8,128)(2,1)}), bf16[16,7,4096]{2,1,0:T(8,128)(2,1)}, u32[]{:S(2)}, u32[]{:S(2)}) async-start(bf16[16,7,4096]{2,1,0:T(8,128)(2,1)} %copy.148), calls=%async_computation.1 | async-start | bytes 2097152 | tf_op jit(solution)/shard_map/all_to_all | solution.py:139
  122.0 0.1 compare_reduce_fusion
  122.1 56.0 %all-to-all-done = bf16[16,7,4096]{2,1,0:T(8,128)(2,1)} async-done(((bf16[16,7,4096]{2,1,0:T(8,128)(2,1)}), bf16[16,7,4096]{2,1,0:T(8,128)(2,1)}, u32[]{:S(2)}, u32[]{:S(2)}) %all-to-all-start) | async-done | bytes 917536 | tf_op jit(solution)/shard_map/all_to_all | solution.py:139
  178.1 3.2 %fusion.39 = f32[8,7,4096]{2,0,1:T(8,128)} fusion(pred[16,8]{0,1:T(8,128)(4,1)S(1)} %compare_reduce_fusion, bf16[2,8,7,4096]{3,2,1,0:T(8,128)(2,1)} %bitcast.74), kind=kOutput, calls=%fused_computation.49 | convolution fusion | flops 7340032 | bytes 1835136 | tf_op jit(solution)/shard_map/dot_general | solution.py:144
  181.3 99.6 %reduce-scatter.2.cloned.1.call-done = bf16[128,3584]{1,0:T(8,128)(2,1)} async-done(((bf16[2048,3584]{1,0:T(8,128)(2,1)}), bf16[128,3584]{1,0:T(8,128)(2,1)}) %reduce-scatter.2.cloned.1.call-update) | async-done | bytes 917520 | tf_op jit(solution)/shard_map/reduce_scatter | solution.py:125
  (46 shorter events, 0.3 us)
Async XLA Ops:
  7.2 72.1 %copy-start = (bf16[448,3584]{1,0:T(8,128)(2,1)S(1)}, bf16[448,3584]{1,0:T(8,128)(2,1)}, u32[]{:S(2)}) copy-start(bf16[448,3584]{1,0:T(8,128)(2,1)} %param.19) | copy-start | bytes 9633796
  7.2 14.7 %copy-start.8 = (f32[1,2048,7]{1,0,2:T(1,128)S(1)}, f32[1,2048,7]{1,0,2:T(1,128)}, u32[]{:S(2)}) copy-start(f32[1,2048,7]{1,0,2:T(1,128)} %param.15) | copy-start | bytes 172036
  7.2 273.7 %reduce-scatter.2.cloned.1.call-start = ((), (), s32[]{:S(2)}) async-start(), calls=%async_computation.2 | async-start | bytes 15597568 | tf_op jit(solution)/shard_map/reduce_scatter | solution.py:125
  13.3 0.6 copy-start.5
  26.6 3.8 %copy-start.7 = (f32[2048,7]{0,1:T(8,128)S(1)}, f32[2048,7]{0,1:T(8,128)}, u32[]{:S(2)}) copy-start(f32[2048,7]{0,1:T(8,128)} %reduce.3) | copy-start | bytes 172036
  26.6 3.8 %copy-start.10 = (f32[8,256]{1,0:T(8,128)S(1)}, f32[8,256]{1,0:T(8,128)}, u32[]{:S(2)}) copy-start(f32[8,256]{1,0:T(8,128)} %get-tuple-element.7) | copy-start | bytes 24580
  26.6 3.8 %copy-start.11 = (f32[8,256]{1,0:T(8,128)S(1)}, f32[8,256]{1,0:T(8,128)}, u32[]{:S(2)}) copy-start(f32[8,256]{1,0:T(8,128)} %get-tuple-element.8) | copy-start | bytes 24580
  26.6 3.9 %copy-start.1 = (bf16[56,8,8,256]{3,2,1,0:T(8,128)(2,1)S(1)}, bf16[56,8,8,256]{3,2,1,0:T(8,128)(2,1)}, u32[]{:S(2)}) copy-start(bf16[56,8,8,256]{3,2,1,0:T(8,128)(2,1)} %copy.177) | copy-start | bytes 5505028
  36.1 6.2 %copy-start.4 = (bf16[1,2048,448]{1,2,0:T(8,128)(2,1)S(1)}, bf16[1,2048,448]{1,2,0:T(8,128)(2,1)}, u32[]{:S(2)}) copy-start(bf16[1,2048,448]{1,2,0:T(8,128)(2,1)} %param.12) | copy-start | bytes 5505028
  45.1 0.7 copy-start.13
  45.1 2.5 copy-start.3
  47.7 0.7 copy-start.16
  53.2 26.1 %copy-start.15 = (f32[448]{0:T(512)S(1)}, f32[448]{0:T(512)}, u32[]{:S(2)}) copy-start(f32[448]{0:T(512)} %param.18) | copy-start | bytes 5380
  94.5 0.7 copy-start.9
  94.5 0.8 copy-start.6
  94.5 2.3 copy-start.2
  103.4 6.5 %copy-start.14 = (s32[8]{0:T(128)S(1)}, s32[8]{0:T(128)}, u32[]{:S(2)}) copy-start(s32[8]{0:T(128)} %get-tuple-element.11) | copy-start | bytes 100
  106.5 15.5 %copy-start.12 = (s32[16,8]{0,1:T(8,128)S(1)}, s32[16,8]{0,1:T(8,128)}, u32[]{:S(2)}) copy-start(s32[16,8]{0,1:T(8,128)} %param.21) | copy-start | bytes 1540
  113.7 64.4 %all-to-all-start = ((bf16[16,7,4096]{2,1,0:T(8,128)(2,1)}), bf16[16,7,4096]{2,1,0:T(8,128)(2,1)}, u32[]{:S(2)}, u32[]{:S(2)}) async-start(bf16[16,7,4096]{2,1,0:T(8,128)(2,1)} %copy.148), calls=%async_computation.1 | async-start | bytes 2097152 | tf_op jit(solution)/shard_map/all_to_all | solution.py:139
Sparse Core Ops, SparseCore 0:
  94.6 186.2 reduce-scatter.1

commit v3 on v2

--- a/solution.py
+++ b/solution.py
@@ -15,6 +15,8 @@
 HIGHEST = lax.Precision.HIGHEST
 TENSOR = ("head_group", "y_rest", "z_hi", "core")
 GROUP_MATES = TENSOR[1:]
+NEAR_FIRST = ("head_group", "y_rest", "core")
+FAR_LAST = "z_hi"
 
 
 def split_pair(values):
@@ -122,12 +124,16 @@
     rounded = (gated * lax.rsqrt(mean_sq + 1e-05)[:, None] * norm_gain[None, :]).astype(
         jnp.bfloat16
     )
-    projected = lax.psum_scatter(
-        jnp.dot(rounded, out_weight, preferred_element_type=jnp.float32).astype(jnp.bfloat16),
-        TENSOR,
-        scatter_dimension=0,
-        tiled=True,
+    sizes = [lax.axis_size(name) for name in TENSOR]
+    rows = stream_len // (sizes[0] * sizes[1] * sizes[2] * sizes[3])
+    reordered = (
+        rounded.reshape(sizes[0], sizes[1], sizes[2], sizes[3], rows, dev_width)
+        .transpose(0, 1, 3, 2, 4, 5)
+        .reshape(stream_len, dev_width)
     )
+    partial = jnp.dot(reordered, out_weight, preferred_element_type=jnp.float32).astype(jnp.bfloat16)
+    near = lax.psum_scatter(partial, NEAR_FIRST, scatter_dimension=0, tiled=True)
+    projected = lax.psum_scatter(near, FAR_LAST, scatter_dimension=0, tiled=True)
     mixed = projected[None]
     dp_idx = lax.axis_index("dp")
     dp_size = lax.axis_size("dp")

time: 288 us -> 299 us (1.038)
  waiting for transfers between devices: 156 us -> 137 us
  local copies, waits for them, and re-layouts: 31.4 us -> 48.3 us
  other arithmetic: 13.4 us -> 23.7 us
    reduce_scatter x1 -> x2, waiting for transfers between devices: 99.6 us -> 84.7 us  [the longest x1 84.7 us: local(): lax.psum_scatter(partial, NEAR_FIRST, scatter_dimension=0, tiled=True)]
    reshape x0 -> x2, local copies, waits for them, and re-layouts: none -> 10.7 us  [the longest x1 5.43 us: local(): mixer_y = outputs.reshape(stream_len, dev_width)]
    convert_element_type x0 -> x1, local copies, waits for them, and re-layouts: none -> 5.75 us  [local(): gated = mixer_y * jax.nn.silu(gate_z[0].astype(jnp.float32))]
    transpose x0 -> x1, other arithmetic: none -> 4.88 us  [local(): reordered = rounded.reshape(sizes[0], sizes[1], sizes[2], sizes[3], rows,...]
    all_to_all x1, waiting for transfers between devices: 56 us -> 52.6 us  [local(): lax.all_to_all(outbound.astype(jnp.bfloat16), 'dp', split_axis=0, concat_...]
    transpose x0 -> x1, local copies, waits for them, and re-layouts: none -> 3.14 us  [local(): reordered = rounded.reshape(sizes[0], sizes[1], sizes[2], sizes[3], rows,...]
    unnamed x49 -> x62, local copies, waits for them, and re-layouts: 13 us -> 12.7 us
  transfers between devices with their start and end apart: 2 -> 3, of which waited for: 2 -> 2; matrix products, arithmetic and copies ran while one was open for 8% -> 8% of each run, Pallas kernels for 0% -> 0%
where the time goes in v3:
time: 299 us; the launch traced here: 297 us
  waiting for transfers between devices  137 us (46%)
  local copies, waits for them, and re-layouts  48.3 us (16%)
  matrix products  44 us (15%)
  other arithmetic  23.7 us (8%)
  blocking collectives  21.5 us (7%)
  between operations  14.5 us (5%)
  starting transfers between devices  8.05 us (3%)
    reduce_scatter x1, waiting for transfers between devices, local(): lax.psum_scatter(partial, NEAR_FIRST, scatter_dimension=0, tiled=True)  84.7 us
    all_to_all x1, waiting for transfers between devices, local(): lax.all_to_all(outbound.astype(jnp.bfloat16), 'dp', split_axis=0, concat_...  52.6 us
    all_gather x1, blocking collectives, local(): group_stat = lax.all_gather(sum_sq, GROUP_MATES, tiled=True)  21.5 us
    dot_general x4, matrix products, split_einsum(): jnp.einsum(form, lower, narrow, preferred_element_type=jnp.float32)  14.1 us
    unnamed x62, local copies, waits for them, and re-layouts  12.7 us
    dot_general x1, matrix products, local(): jnp.dot(reordered, out_weight, preferred_element_type=jnp.float32)  12.6 us
    dot_general x4, matrix products, split_einsum(): first = jnp.einsum(form, upper, narrow, preferred_element_type=jnp.float32)  9.01 us
    all_to_all x1, starting transfers between devices, local(): lax.all_to_all(outbound.astype(jnp.bfloat16), 'dp', split_axis=0, concat_...  7.75 us
  transfers between devices with their start and end apart: 3, of which 2 were waited for; matrix products, arithmetic and copies ran while one was open for 8% of the time, Pallas kernels for 0%

profile of v3, /device:TPU:32, one launch (start us, length us, event | category | flops | bytes accessed | tf_op | source)
XLA Modules:
  0.0 297.4 jit_solution(11815457912186518607)
XLA Ops:
  7.2 0.5 broadcast.237
  7.8 1.4 reduce.9
  9.3 0.7 neg.23
  10.0 0.9 multiply_bitcast_fusion
  10.9 2.0 reduce-window.6
  12.9 0.2 slice_reduce_fusion
  13.1 0.2 reduce-window.9
  13.2 0.1 add_bitcast_fusion
  13.3 0.6 copy-done.8
  14.1 0.1 copy.245
  14.3 0.9 dynamic-slice_reduce_fusion
  15.2 0.6 and_select_fusion
  15.8 0.7 compare_convert_fusion
  16.5 0.7 fusion.50
  17.1 0.6 copy.328
  17.8 0.6 iota_compare_fusion
  18.4 3.3 %copy.253 = bf16[56,8,8,256]{3,2,1,0:T(8,128)(2,1)} copy(bf16[56,8,8,256]{3,1,2,0:T(8,128)(2,1)} %bitcast.154) | data formatting | bytes 3670016
  21.7 0.1 copy.246
  21.9 0.8 reduce.3
  22.6 0.1 copy.247
  22.8 2.5 constant_dynamic-slice_fusion
  25.3 1.2 copy.243
  26.6 1.0 copy.193
  27.7 1.3 compare_and_fusion
  29.0 1.5 fusion.38
  30.5 0.7 exponential_multiply_fusion
  31.2 6.6 %fusion.4 = f32[8,7,256,64]{2,3,1,0:T(8,128)} fusion(f32[8,256,256]{2,1,0:T(8,128)S(1)} %fusion.38, f32[8,7,256]{2,1,0:T(8,128)S(1)} %get-tuple-element.6, f32[8,7,256]{2,1,0:T(8,128)S(1)} %copy.193, pred[8,256,256]{2,1,0:T(8,128)(4,1)S(1)} %compare_and_fusion, bf16[8,256,7,64]{1,0,3,2:T(8,128)(2,1)S(1)} %bitcast.148), kind=kOutput, calls=%fused_computation.7 | convolution fusion | flops 488112128 | bytes 8241152 | tf_op jit(solution)/shard_map/bhts,bshp->bthp/dot_general | solution.py:30
  37.8 6.9 %fusion.1 = f32[8,7,256,64]{2,3,1,0:T(8,128)} fusion(f32[8,256,256]{2,1,0:T(8,128)S(1)} %fusion.38, f32[8,7,256]{2,1,0:T(8,128)S(1)} %get-tuple-element.6, f32[8,7,256]{2,1,0:T(8,128)S(1)} %copy.193, pred[8,256,256]{2,1,0:T(8,128)(4,1)S(1)} %compare_and_fusion, bf16[8,256,7,64]{1,0,3,2:T(8,128)(2,1)S(1)} %bitcast.149), kind=kOutput, calls=%fused_computation.5 | convolution fusion | flops 499122176 | bytes 8241152 | tf_op jit(solution)/shard_map/bhts,bshp->bthp/dot_general | solution.py:31
  44.7 2.4 convert_element_type.182
  47.1 5.7 %reshape.356 = f32[2,2,2,2,128,448]{4,3,2,1,0,5:T(2,128)} reshape(bf16[1,2048,448]{1,2,0:T(8,128)(2,1)} %param.12) | data formatting | bytes 5505024 | tf_op jit(solution)/shard_map/convert_element_type | solution.py:120
  52.8 3.9 %copy.254 = f32[56,8,8,256]{3,2,1,0:T(8,128)S(1)} copy(f32[56,8,8,256]{3,1,2,0:T(8,128)} %bitcast.147) | data formatting | bytes 7340032
  56.7 0.7 fusion.18
  57.4 0.6 fusion.25
  58.1 0.1 select_exponential_fusion
  58.2 1.8 multiply_reduce_fusion
  60.0 0.6 fusion.36
  60.6 0.2 copy-done.14
  60.9 1.2 copy-done.22
  62.1 4.5 %multiply_reduce_fusion.1 = (f32[8,256]{1,0:T(8,128)S(1)}, f32[8,256,7,64]{1,3,2,0:T(8,128)}) fusion(f32[8,256,7,64]{1,0,3,2:T(8,128)S(1)} %bitcast.159, bf16[8,256,7,64]{1,0,3,2:T(8,128)(2,1)S(1)} %bitcast.152, f32[7]{0:T(128)S(1)} %copy-done.21, f32[8,256,7]{1,2,0:T(8,128)S(1)} %copy-done.14, f32[8,256,7,64]{1,3,2,0:T(8,128)S(1)} %fusion.36, ...), kind=kOutput, calls=%fused_computation.24 | convolution fusion | flops 131201024 | bytes 21430300 | tf_op jit(solution)/shard_map/bhpn,btn->bthp/dot_general | solution.py:31
  66.6 21.5 %all_gather.3 = f32[16384]{0:T(1024)} all-gather(f32[2048]{0:T(1024)S(1)} %bitcast.183), channel_id=1, replica_groups=mesh['dp'=16,'head_group'=2,'y_rest'=2,'z_hi'=2,'core'=2] {'y_rest','z_h..., dimensions={0}, use_global_device_ids=true | all-gather | bytes 73728 | tf_op jit(solution)/shard_map/all_gather | solution.py:122
  88.1 0.9 reshape.351
  89.0 5.4 %reshape.350 = f32[2,2,2,2,128,448]{4,3,5,2,1,0:T(2,128)} reshape(f32[8,256,7,64]{1,3,2,0:T(8,128)} %get-tuple-element.10) | data formatting | bytes 7340032 | tf_op jit(solution)/shard_map/reshape | solution.py:97
  94.4 4.9 %fusion.24 = bf16[2,2,2,2,128,448]{4,5,2,3,1,0:T(8,128)(2,1)S(1)} fusion(f32[448]{0:T(512)S(1)} %copy-done.19, f32[2,2,2,2,128]{4,3,2,1,0:T(2,128)S(1)} %bitcast.184, f32[2,2,2,2,128,448]{4,3,2,1,0,5:T(2,128)} %reshape.356, f32[2,2,2,2,128,448]{4,3,5,2,1,0:T(2,128)} %reshape.350), kind=kLoop, calls=%fused_computation.34 | loop fusion | flops 7340032 | bytes 9185024 | tf_op jit(solution)/shard_map/transpose | solution.py:131
  99.3 3.1 %copy.222 = bf16[2,2,2,2,128,448]{4,3,2,1,0,5:T(2,128)(2,1)} copy(bf16[2,2,2,2,128,448]{4,5,2,3,1,0:T(8,128)(2,1)S(1)} %fusion.24) | data formatting | bytes 3670016 | tf_op jit(solution)/shard_map/transpose | solution.py:131
  102.5 5.3 %reshape.352 = bf16[2048,448]{0,1:T(8,128)(2,1)} reshape(bf16[2,2,2,2,128,448]{4,3,2,1,0,5:T(2,128)(2,1)} %copy.222) | data formatting | bytes 3670016 | tf_op jit(solution)/shard_map/reshape | solution.py:132
  107.7 12.6 %convolution_convert_fusion = bf16[2048,3584]{1,0:T(8,128)(2,1)} fusion(bf16[2048,448]{0,1:T(8,128)(2,1)} %reshape.352, bf16[448,3584]{1,0:T(8,128)(2,1)S(1)} %copy-done), kind=kOutput, calls=%fused_computation | convolution fusion | flops 6584008704 | bytes 19726336 | tf_op jit(solution)/shard_map/dot_general | solution.py:134
  120.3 0.3 reduce-scatter.5.cloned.1.call-start
  120.6 0.4 copy-done.13
  121.0 0.1 convert_reduce_fusion
  121.2 0.2 fusion.46
  121.4 1.5 broadcast_multiply_fusion
  122.9 84.7 %reduce-scatter.3.cloned.1.call-done = bf16[256,3584]{1,0:T(8,128)(2,1)} async-done(((bf16[2048,3584]{1,0:T(8,128)(2,1)}), bf16[256,3584]{1,0:T(8,128)(2,1)}) %reduce-scatter.3.cloned.1.call-update) | async-done | bytes 1835024 | tf_op jit(solution)/shard_map/reduce_scatter | solution.py:135
  207.7 1.2 fusion.17
  208.9 2.3 fusion.12
  211.2 1.1 fusion.57
  212.3 2.1 convolution_add_fusion
  214.4 2.6 reshape.353
  217.0 3.1 %copy.324 = f32[7,64,8,64]{3,1,0,2:T(8,128)} copy(f32[7,64,8,64]{3,2,1,0:T(8,128)} %reshape.353) | data formatting | bytes 1835008 | tf_op jit(solution)/shard_map/reshape | solution.py:116
  220.1 3.0 %reshape.354 = f32[8,28672]{1,0:T(8,128)} reshape(f32[8,7,64,64]{3,2,1,0:T(8,128)} %bitcast.153) | data formatting | bytes 1835008 | tf_op jit(solution)/shard_map/reshape | solution.py:118
  223.1 2.2 convolution_convert_fusion.1
  225.3 1.5 copy.224
  226.8 7.7 %all-to-all-start = ((bf16[16,7,4096]{2,1,0:T(8,128)(2,1)}), bf16[16,7,4096]{2,1,0:T(8,128)(2,1)}, u32[]{:S(2)}, u32[]{:S(2)}) async-start(bf16[16,7,4096]{2,1,0:T(8,128)(2,1)} %copy.224), calls=%async_computation.2 | async-start | bytes 2097152 | tf_op jit(solution)/shard_map/all_to_all | solution.py:145
  234.7 52.6 %all-to-all-done = bf16[16,7,4096]{2,1,0:T(8,128)(2,1)} async-done(((bf16[16,7,4096]{2,1,0:T(8,128)(2,1)}), bf16[16,7,4096]{2,1,0:T(8,128)(2,1)}, u32[]{:S(2)}, u32[]{:S(2)}) %all-to-all-start) | async-done | bytes 917536 | tf_op jit(solution)/shard_map/all_to_all | solution.py:145
  287.3 3.2 %fusion.32 = f32[8,7,4096]{2,0,1:T(8,128)} fusion(pred[16,8]{0,1:T(8,128)(4,1)S(1)} %compare_reduce_fusion, bf16[2,8,7,4096]{3,2,1,0:T(8,128)(2,1)} %bitcast.74), kind=kOutput, calls=%fused_computation.42 | convolution fusion | flops 7340032 | bytes 1835136 | tf_op jit(solution)/shard_map/dot_general | solution.py:150
  (66 shorter events, 0.9 us)
Async XLA Ops:
  7.2 100.6 %copy-start = (bf16[448,3584]{1,0:T(8,128)(2,1)S(1)}, bf16[448,3584]{1,0:T(8,128)(2,1)}, u32[]{:S(2)}) copy-start(bf16[448,3584]{1,0:T(8,128)(2,1)} %param.19) | copy-start | bytes 9633796
  7.2 14.7 %copy-start.12 = (f32[1,2048,7]{1,0,2:T(1,128)S(1)}, f32[1,2048,7]{1,0,2:T(1,128)}, u32[]{:S(2)}) copy-start(f32[1,2048,7]{1,0,2:T(1,128)} %param.15) | copy-start | bytes 172036
  7.2 200.4 %reduce-scatter.3.cloned.1.call-start = ((), (), s32[]{:S(2)}) async-start(), calls=%async_computation.3 | async-start | bytes 16515072 | tf_op jit(solution)/shard_map/reduce_scatter | solution.py:135
  13.3 0.6 copy-start.8
  26.5 3.9 %copy-start.11 = (f32[2048,7]{0,1:T(8,128)S(1)}, f32[2048,7]{0,1:T(8,128)}, u32[]{:S(2)}) copy-start(f32[2048,7]{0,1:T(8,128)} %reduce.3) | copy-start | bytes 172036
  26.5 3.9 %copy-start.15 = (f32[8,256]{1,0:T(8,128)S(1)}, f32[8,256]{1,0:T(8,128)}, u32[]{:S(2)}) copy-start(f32[8,256]{1,0:T(8,128)} %get-tuple-element.7) | copy-start | bytes 24580
  26.5 3.9 %copy-start.16 = (f32[8,256]{1,0:T(8,128)S(1)}, f32[8,256]{1,0:T(8,128)}, u32[]{:S(2)}) copy-start(f32[8,256]{1,0:T(8,128)} %get-tuple-element.8) | copy-start | bytes 24580
  26.6 4.6 %copy-start.1 = (bf16[56,8,8,256]{3,2,1,0:T(8,128)(2,1)S(1)}, bf16[56,8,8,256]{3,2,1,0:T(8,128)(2,1)}, u32[]{:S(2)}) copy-start(bf16[56,8,8,256]{3,2,1,0:T(8,128)(2,1)} %copy.253) | copy-start | bytes 5505028
  26.6 2.3 copy-start.5
  37.8 6.9 %copy-start.3 = (bf16[1,2048,448]{1,2,0:T(8,128)(2,1)S(1)}, bf16[1,2048,448]{1,2,0:T(8,128)(2,1)}, u32[]{:S(2)}) copy-start(bf16[1,2048,448]{1,2,0:T(8,128)(2,1)} %param.12) | copy-start | bytes 5505028
  52.8 3.9 %copy-start.2 = (bf16[56,8,8,256]{3,2,1,0:T(8,128)(2,1)S(1)}, bf16[56,8,8,256]{3,2,1,0:T(8,128)(2,1)}, u32[]{:S(2)}) copy-start(bf16[56,8,8,256]{3,2,1,0:T(8,128)(2,1)} %copy.253) | copy-start | bytes 5505028
  52.8 3.9 %copy-start.6 = (bf16[8,8,8,256]{3,2,1,0:T(8,128)(2,1)S(1)}, bf16[8,8,8,256]{3,2,1,0:T(8,128)(2,1)}, u32[]{:S(2)}) copy-start(bf16[8,8,8,256]{3,2,1,0:T(8,128)(2,1)} %copy-done.5) | copy-start | bytes 786436
  52.8 3.9 %copy-start.10 = (f32[8,256,7]{1,2,0:T(8,128)S(1)}, f32[8,256,7]{1,2,0:T(8,128)}, u32[]{:S(2)}) copy-start(f32[8,256,7]{1,2,0:T(8,128)} %get-tuple-element.5) | copy-start | bytes 172036
  57.4 0.7 copy-start.18
  57.4 2.6 copy-start.4
  58.2 2.5 copy-start.23
  59.9 0.9 copy-start.14
  59.9 0.9 copy-start.21
  60.0 2.1 copy-start.22
  89.0 5.4 %copy-start.19 = (f32[448]{0:T(512)S(1)}, f32[448]{0:T(512)}, u32[]{:S(2)}) copy-start(f32[448]{0:T(512)} %param.18) | copy-start | bytes 5380
  120.3 0.7 copy-start.13
  120.3 0.8 copy-start.9
  120.3 170.2 %reduce-scatter.5.cloned.1.call-start = ((), (), s32[]{:S(2)}) async-start(), calls=%async_computation.4 | async-start | bytes 2752512 | tf_op jit(solution)/shard_map/reduce_scatter | solution.py:136
  207.6 3.5 %copy-start.7 = (bf16[2048,8,64]{0,2,1:T(8,128)(2,1)S(1)}, bf16[2048,8,64]{0,2,1:T(8,128)(2,1)}, u32[]{:S(2)}) copy-start(bf16[2048,8,64]{0,2,1:T(8,128)(2,1)} %broadcast_multiply_fusion) | copy-start | bytes 6291460
  217.0 6.1 %copy-start.20 = (s32[8]{0:T(128)S(1)}, s32[8]{0:T(128)}, u32[]{:S(2)}) copy-start(s32[8]{0:T(128)} %get-tuple-element.11) | copy-start | bytes 100
  220.1 14.5 %copy-start.17 = (s32[16,8]{0,1:T(8,128)S(1)}, s32[16,8]{0,1:T(8,128)}, u32[]{:S(2)}) copy-start(s32[16,8]{0,1:T(8,128)} %param.21) | copy-start | bytes 1540
  226.8 60.5 %all-to-all-start = ((bf16[16,7,4096]{2,1,0:T(8,128)(2,1)}), bf16[16,7,4096]{2,1,0:T(8,128)(2,1)}, u32[]{:S(2)}, u32[]{:S(2)}) async-start(bf16[16,7,4096]{2,1,0:T(8,128)(2,1)} %copy.224), calls=%async_computation.2 | async-start | bytes 2097152 | tf_op jit(solution)/shard_map/all_to_all | solution.py:145
Sparse Core Ops, SparseCore 0:
  120.5 87.1 reduce-scatter.2
  210.7 70.8 reduce-scatter.4

commit v4 on v3

--- a/solution.py
+++ b/solution.py
@@ -133,8 +133,7 @@
     )
     partial = jnp.dot(reordered, out_weight, preferred_element_type=jnp.float32).astype(jnp.bfloat16)
     near = lax.psum_scatter(partial, NEAR_FIRST, scatter_dimension=0, tiled=True)
-    projected = lax.psum_scatter(near, FAR_LAST, scatter_dimension=0, tiled=True)
-    mixed = projected[None]
+    mixed = near
     dp_idx = lax.axis_index("dp")
     dp_size = lax.axis_size("dp")
     own_slots = lax.dynamic_slice_in_dim(cache_slot, dp_idx, 1, 0)[0]
@@ -145,6 +144,9 @@
     inbound = lax.all_to_all(
         outbound.astype(jnp.bfloat16), "dp", split_axis=0, concat_axis=0, tiled=True
     ).astype(outbound.dtype)
+    near, inbound = lax.optimization_barrier((mixed, inbound))
+    projected = lax.psum_scatter(near, FAR_LAST, scatter_dimension=0, tiled=True)
+    mixed = projected[None]
     wanted = dp_idx * REQS + jnp.arange(REQS)
     take_hot = jnp.any(cache_slot[:, :, None] == wanted[None, None, :], axis=1).astype(jnp.float32)
     cache = jnp.dot(

time: 299 us -> 277 us (0.926)
  waiting for transfers between devices: 137 us -> 88.7 us
  blocking collectives: 21.5 us -> 56.3 us
  starting transfers between devices: 8.05 us -> 0.3 us
    reduce_scatter x1, waiting for transfers between devices: 0.01 us -> 55.6 us  [local(): lax.psum_scatter(near, FAR_LAST, scatter_dimension=0, tiled=True)]
    all_to_all x1 -> x0, waiting for transfers between devices: 52.6 us -> none  [local(): lax.all_to_all(outbound.astype(jnp.bfloat16), 'dp', split_axis=0, concat_...]
    reduce_scatter x1, waiting for transfers between devices: 84.7 us -> 33.1 us  [local(): lax.psum_scatter(partial, NEAR_FIRST, scatter_dimension=0, tiled=True)]
    all_to_all x0 -> x1, blocking collectives: none -> 34.8 us  [local(): lax.all_to_all(outbound.astype(jnp.bfloat16), 'dp', split_axis=0, concat_...]
    all_to_all x1 -> x0, starting transfers between devices: 7.75 us -> none  [local(): lax.all_to_all(outbound.astype(jnp.bfloat16), 'dp', split_axis=0, concat_...]
  transfers between devices with their start and end apart: 3 -> 2, of which waited for: 2 -> 2; matrix products, arithmetic and copies ran while one was open for 8% -> 8% of each run, Pallas kernels for 0% -> 0%
where the time goes in v4:
time: 277 us; the launch traced here: 274 us
  waiting for transfers between devices  88.7 us (32%)
  blocking collectives  56.3 us (20%)
  local copies, waits for them, and re-layouts  47.3 us (17%)
  matrix products  45 us (16%)
  other arithmetic  22.3 us (8%)
  between operations  14.5 us (5%)
    reduce_scatter x1, waiting for transfers between devices, local(): lax.psum_scatter(near, FAR_LAST, scatter_dimension=0, tiled=True)  55.6 us
    all_to_all x1, blocking collectives, local(): lax.all_to_all(outbound.astype(jnp.bfloat16), 'dp', split_axis=0, concat_...  34.8 us
    reduce_scatter x1, waiting for transfers between devices, local(): lax.psum_scatter(partial, NEAR_FIRST, scatter_dimension=0, tiled=True)  33.1 us
    all_gather x1, blocking collectives, local(): group_stat = lax.all_gather(sum_sq, GROUP_MATES, tiled=True)  21.5 us
    dot_general x4, matrix products, split_einsum(): jnp.einsum(form, lower, narrow, preferred_element_type=jnp.float32)  14.1 us
    unnamed x62, local copies, waits for them, and re-layouts  12.7 us
    dot_general x1, matrix products, local(): jnp.dot(reordered, out_weight, preferred_element_type=jnp.float32)  12.6 us
    dot_general x4, matrix products, split_einsum(): first = jnp.einsum(form, upper, narrow, preferred_element_type=jnp.float32)  9.08 us
  transfers between devices with their start and end apart: 2, of which 2 were waited for; matrix products, arithmetic and copies ran while one was open for 8% of the time, Pallas kernels for 0%

profile of v4, /device:TPU:32, one launch (start us, length us, event | category | flops | bytes accessed | tf_op | source)
XLA Modules:
  0.0 274.4 jit_solution(6131530091263890229)
XLA Ops:
  7.2 0.5 broadcast.237
  7.8 1.4 reduce.9
  9.3 0.7 neg.23
  10.0 0.9 multiply_bitcast_fusion
  10.9 2.0 reduce-window.6
  12.9 0.2 slice_reduce_fusion
  13.1 0.2 reduce-window.9
  13.3 0.6 copy-done.8
  14.2 0.1 copy.245
  14.3 0.9 dynamic-slice_reduce_fusion
  15.2 0.6 and_select_fusion
  15.8 0.7 compare_convert_fusion
  16.5 0.6 fusion.50
  17.1 0.6 copy.328
  17.7 0.6 iota_compare_fusion
  18.4 3.3 %copy.253 = bf16[56,8,8,256]{3,2,1,0:T(8,128)(2,1)} copy(bf16[56,8,8,256]{3,1,2,0:T(8,128)(2,1)} %bitcast.155) | data formatting | bytes 3670016
  21.7 0.1 copy.246
  21.9 0.8 reduce.3
  22.6 0.1 copy.247
  22.8 2.6 constant_dynamic-slice_fusion
  25.3 1.2 copy.243
  26.7 1.0 copy.193
  27.7 1.3 compare_and_fusion
  29.0 1.5 fusion.38
  30.5 0.7 exponential_multiply_fusion
  31.2 6.6 %fusion.4 = f32[8,7,256,64]{2,3,1,0:T(8,128)} fusion(f32[8,256,256]{2,1,0:T(8,128)S(1)} %fusion.38, f32[8,7,256]{2,1,0:T(8,128)S(1)} %get-tuple-element.10, f32[8,7,256]{2,1,0:T(8,128)S(1)} %copy.193, pred[8,256,256]{2,1,0:T(8,128)(4,1)S(1)} %compare_and_fusion, bf16[8,256,7,64]{1,0,3,2:T(8,128)(2,1)S(1)} %bitcast.149), kind=kOutput, calls=%fused_computation.7 | convolution fusion | flops 488112128 | bytes 8241152 | tf_op jit(solution)/shard_map/bhts,bshp->bthp/dot_general | solution.py:30
  37.9 6.9 %fusion.1 = f32[8,7,256,64]{2,3,1,0:T(8,128)} fusion(f32[8,256,256]{2,1,0:T(8,128)S(1)} %fusion.38, f32[8,7,256]{2,1,0:T(8,128)S(1)} %get-tuple-element.10, f32[8,7,256]{2,1,0:T(8,128)S(1)} %copy.193, pred[8,256,256]{2,1,0:T(8,128)(4,1)S(1)} %compare_and_fusion, bf16[8,256,7,64]{1,0,3,2:T(8,128)(2,1)S(1)} %bitcast.150), kind=kOutput, calls=%fused_computation.5 | convolution fusion | flops 499122176 | bytes 8241152 | tf_op jit(solution)/shard_map/bhts,bshp->bthp/dot_general | solution.py:31
  44.8 2.3 convert_element_type.185
  47.1 5.7 %reshape.356 = f32[2,2,2,2,128,448]{4,3,2,1,0,5:T(2,128)} reshape(bf16[1,2048,448]{1,2,0:T(8,128)(2,1)} %param.12) | data formatting | bytes 5505024 | tf_op jit(solution)/shard_map/convert_element_type | solution.py:120
  52.8 3.9 %copy.254 = f32[56,8,8,256]{3,2,1,0:T(8,128)S(1)} copy(f32[56,8,8,256]{3,1,2,0:T(8,128)} %bitcast.147) | data formatting | bytes 7340032
  56.7 0.7 fusion.18
  57.4 0.6 fusion.28
  58.1 0.1 select_exponential_fusion
  58.1 1.8 multiply_reduce_fusion
  60.0 0.6 fusion.36
  60.6 0.2 copy-done.14
  60.8 1.2 copy-done.22
  62.1 4.5 %multiply_reduce_fusion.1 = (f32[8,256]{1,0:T(8,128)S(1)}, f32[8,256,7,64]{1,3,2,0:T(8,128)}) fusion(f32[8,256,7,64]{1,0,3,2:T(8,128)S(1)} %bitcast.160, bf16[8,256,7,64]{1,0,3,2:T(8,128)(2,1)S(1)} %bitcast.153, f32[7]{0:T(128)S(1)} %copy-done.21, f32[8,256,7]{1,2,0:T(8,128)S(1)} %copy-done.14, f32[8,256,7,64]{1,3,2,0:T(8,128)S(1)} %fusion.36, ...), kind=kOutput, calls=%fused_computation.24 | convolution fusion | flops 131201024 | bytes 21430300 | tf_op jit(solution)/shard_map/bhpn,btn->bthp/dot_general | solution.py:31
  66.6 21.5 %all_gather.3 = f32[16384]{0:T(1024)} all-gather(f32[2048]{0:T(1024)S(1)} %bitcast.184), channel_id=1, replica_groups=mesh['dp'=16,'head_group'=2,'y_rest'=2,'z_hi'=2,'core'=2] {'y_rest','z_h..., dimensions={0}, use_global_device_ids=true | all-gather | bytes 73728 | tf_op jit(solution)/shard_map/all_gather | solution.py:122
  88.1 0.9 reshape.351
  89.0 5.4 %reshape.350 = f32[2,2,2,2,128,448]{4,3,5,2,1,0:T(2,128)} reshape(f32[8,256,7,64]{1,3,2,0:T(8,128)} %get-tuple-element.14) | data formatting | bytes 7340032 | tf_op jit(solution)/shard_map/reshape | solution.py:97
  94.4 4.9 %fusion.27 = bf16[2,2,2,2,128,448]{4,5,2,3,1,0:T(8,128)(2,1)S(1)} fusion(f32[448]{0:T(512)S(1)} %copy-done.19, f32[2,2,2,2,128]{4,3,2,1,0:T(2,128)S(1)} %bitcast.185, f32[2,2,2,2,128,448]{4,3,2,1,0,5:T(2,128)} %reshape.356, f32[2,2,2,2,128,448]{4,3,5,2,1,0:T(2,128)} %reshape.350), kind=kLoop, calls=%fused_computation.37 | loop fusion | flops 7340032 | bytes 9185024 | tf_op jit(solution)/shard_map/transpose | solution.py:131
  99.3 3.1 %copy.222 = bf16[2,2,2,2,128,448]{4,3,2,1,0,5:T(2,128)(2,1)} copy(bf16[2,2,2,2,128,448]{4,5,2,3,1,0:T(8,128)(2,1)S(1)} %fusion.27) | data formatting | bytes 3670016 | tf_op jit(solution)/shard_map/transpose | solution.py:131
  102.4 5.3 %reshape.352 = bf16[2048,448]{0,1:T(8,128)(2,1)} reshape(bf16[2,2,2,2,128,448]{4,3,2,1,0,5:T(2,128)(2,1)} %copy.222) | data formatting | bytes 3670016 | tf_op jit(solution)/shard_map/reshape | solution.py:132
  107.7 12.6 %convolution_convert_fusion = bf16[2048,3584]{1,0:T(8,128)(2,1)} fusion(bf16[2048,448]{0,1:T(8,128)(2,1)} %reshape.352, bf16[448,3584]{1,0:T(8,128)(2,1)S(1)} %copy-done), kind=kOutput, calls=%fused_computation | convolution fusion | flops 6584008704 | bytes 19726336 | tf_op jit(solution)/shard_map/dot_general | solution.py:134
  120.4 0.3 reduce-scatter.5.cloned.1.call-start
  120.7 0.4 copy-done.13
  121.0 0.1 convert_reduce_fusion
  121.2 0.2 fusion.46
  121.4 1.1 fusion.17
  122.5 0.2 broadcast_multiply_fusion
  122.7 0.7 fusion.12
  123.4 1.1 fusion.57
  124.6 2.1 convolution_add_fusion
  126.7 2.6 reshape.353
  129.3 3.1 %copy.324 = f32[7,64,8,64]{3,1,0,2:T(8,128)} copy(f32[7,64,8,64]{3,2,1,0:T(8,128)} %reshape.353) | data formatting | bytes 1835008 | tf_op jit(solution)/shard_map/reshape | solution.py:116
  132.4 3.0 %reshape.354 = f32[8,28672]{1,0:T(8,128)} reshape(f32[8,7,64,64]{3,2,1,0:T(8,128)} %bitcast.154) | data formatting | bytes 1835008 | tf_op jit(solution)/shard_map/reshape | solution.py:118
  135.4 2.3 convolution_convert_fusion.1
  137.6 0.5 copy.224
  138.2 34.8 %all_to_all.5 = bf16[16,7,4096]{2,1,0:T(8,128)(2,1)S(1)} all-to-all(bf16[16,7,4096]{2,1,0:T(8,128)(2,1)S(1)} %copy.224), channel_id=1, replica_groups=mesh['dp'=16,'head_group'=2,'y_rest'=2,'z_hi'=2,'core'=2] {'dp'}, dimensions={0} | all-to-all | bytes 1835008 | tf_op jit(solution)/shard_map/all_to_all | solution.py:144
  173.0 1.5 convert_element_type.184
  174.6 33.1 %reduce-scatter.3.cloned.1.call-done = bf16[256,3584]{1,0:T(8,128)(2,1)} async-done(((bf16[2048,3584]{1,0:T(8,128)(2,1)}), bf16[256,3584]{1,0:T(8,128)(2,1)}) %reduce-scatter.3.cloned.1.call-update) | async-done | bytes 1835024 | tf_op jit(solution)/shard_map/reduce_scatter | solution.py:135
  207.8 4.2 %fusion.20 = f32[8,7,4096]{2,0,1:T(8,128)} fusion(pred[16,8]{0,1:T(8,128)(4,1)S(1)} %compare_reduce_fusion, f32[2,8,7,4096]{3,2,1,0:T(8,128)} %bitcast.148), kind=kOutput, calls=%fused_computation.30 | convolution fusion | flops 44040192 | bytes 2752640 | tf_op jit(solution)/shard_map/dot_general | solution.py:152
  212.0 55.6 %reduce-scatter.5.cloned.1.call-done = bf16[128,3584]{1,0:T(8,128)(2,1)} async-done(((bf16[256,3584]{1,0:T(8,128)(2,1)}), bf16[128,3584]{1,0:T(8,128)(2,1)}) %reduce-scatter.5.cloned.1.call-update) | async-done | bytes 917520 | tf_op jit(solution)/shard_map/reduce_scatter | solution.py:148
  (66 shorter events, 0.9 us)
Async XLA Ops:
  7.2 100.6 %copy-start = (bf16[448,3584]{1,0:T(8,128)(2,1)S(1)}, bf16[448,3584]{1,0:T(8,128)(2,1)}, u32[]{:S(2)}) copy-start(bf16[448,3584]{1,0:T(8,128)(2,1)} %param.19) | copy-start | bytes 9633796
  7.2 14.7 %copy-start.12 = (f32[1,2048,7]{1,0,2:T(1,128)S(1)}, f32[1,2048,7]{1,0,2:T(1,128)}, u32[]{:S(2)}) copy-start(f32[1,2048,7]{1,0,2:T(1,128)} %param.15) | copy-start | bytes 172036
  7.2 200.5 %reduce-scatter.3.cloned.1.call-start = ((), (), s32[]{:S(2)}) async-start(), calls=%async_computation.3 | async-start | bytes 16515072 | tf_op jit(solution)/shard_map/reduce_scatter | solution.py:135
  13.3 0.6 copy-start.8
  26.6 3.9 %copy-start.11 = (f32[2048,7]{0,1:T(8,128)S(1)}, f32[2048,7]{0,1:T(8,128)}, u32[]{:S(2)}) copy-start(f32[2048,7]{0,1:T(8,128)} %reduce.3) | copy-start | bytes 172036
  26.6 3.9 %copy-start.15 = (f32[8,256]{1,0:T(8,128)S(1)}, f32[8,256]{1,0:T(8,128)}, u32[]{:S(2)}) copy-start(f32[8,256]{1,0:T(8,128)} %get-tuple-element.11) | copy-start | bytes 24580
  26.6 3.9 %copy-start.16 = (f32[8,256]{1,0:T(8,128)S(1)}, f32[8,256]{1,0:T(8,128)}, u32[]{:S(2)}) copy-start(f32[8,256]{1,0:T(8,128)} %get-tuple-element.12) | copy-start | bytes 24580
  26.6 4.7 %copy-start.1 = (bf16[56,8,8,256]{3,2,1,0:T(8,128)(2,1)S(1)}, bf16[56,8,8,256]{3,2,1,0:T(8,128)(2,1)}, u32[]{:S(2)}) copy-start(bf16[56,8,8,256]{3,2,1,0:T(8,128)(2,1)} %copy.253) | copy-start | bytes 5505028
  26.7 2.3 copy-start.6
  37.9 6.9 %copy-start.4 = (bf16[1,2048,448]{1,2,0:T(8,128)(2,1)S(1)}, bf16[1,2048,448]{1,2,0:T(8,128)(2,1)}, u32[]{:S(2)}) copy-start(bf16[1,2048,448]{1,2,0:T(8,128)(2,1)} %param.12) | copy-start | bytes 5505028
  52.8 3.9 %copy-start.2 = (bf16[56,8,8,256]{3,2,1,0:T(8,128)(2,1)S(1)}, bf16[56,8,8,256]{3,2,1,0:T(8,128)(2,1)}, u32[]{:S(2)}) copy-start(bf16[56,8,8,256]{3,2,1,0:T(8,128)(2,1)} %copy.253) | copy-start | bytes 5505028
  52.8 3.9 %copy-start.7 = (bf16[8,8,8,256]{3,2,1,0:T(8,128)(2,1)S(1)}, bf16[8,8,8,256]{3,2,1,0:T(8,128)(2,1)}, u32[]{:S(2)}) copy-start(bf16[8,8,8,256]{3,2,1,0:T(8,128)(2,1)} %copy-done.6) | copy-start | bytes 786436
  52.8 3.9 %copy-start.10 = (f32[8,256,7]{1,2,0:T(8,128)S(1)}, f32[8,256,7]{1,2,0:T(8,128)}, u32[]{:S(2)}) copy-start(f32[8,256,7]{1,2,0:T(8,128)} %get-tuple-element.9) | copy-start | bytes 172036
  57.4 0.7 copy-start.18
  57.4 2.6 copy-start.5
  58.1 2.5 copy-start.23
  59.9 0.9 copy-start.14
  59.9 0.9 copy-start.21
  59.9 2.1 copy-start.22
  89.0 5.4 %copy-start.19 = (f32[448]{0:T(512)S(1)}, f32[448]{0:T(512)}, u32[]{:S(2)}) copy-start(f32[448]{0:T(512)} %param.18) | copy-start | bytes 5380
  120.3 0.7 copy-start.13
  120.3 0.8 copy-start.9
  120.4 147.2 %reduce-scatter.5.cloned.1.call-start = ((), (), s32[]{:S(2)}) async-start(), calls=%async_computation.4 | async-start | bytes 2752512 | tf_op jit(solution)/shard_map/reduce_scatter | solution.py:148
  120.6 2.0 copy-start.3
  129.3 6.1 %copy-start.20 = (s32[8]{0:T(128)S(1)}, s32[8]{0:T(128)}, u32[]{:S(2)}) copy-start(s32[8]{0:T(128)} %get-tuple-element.15) | copy-start | bytes 100
  138.2 69.6 %copy-start.17 = (s32[16,8]{0,1:T(8,128)S(1)}, s32[16,8]{0,1:T(8,128)}, u32[]{:S(2)}) copy-start(s32[16,8]{0,1:T(8,128)} %param.21) | copy-start | bytes 1540
Sparse Core Ops, SparseCore 0:
  120.5 87.1 reduce-scatter.2
  210.8 56.7 reduce-scatter.4

commit v5 on v4

--- a/solution.py
+++ b/solution.py
@@ -145,7 +145,12 @@
         outbound.astype(jnp.bfloat16), "dp", split_axis=0, concat_axis=0, tiled=True
     ).astype(outbound.dtype)
     near, inbound = lax.optimization_barrier((mixed, inbound))
-    projected = lax.psum_scatter(near, FAR_LAST, scatter_dimension=0, tiled=True)
+    far_idx = lax.axis_index(FAR_LAST)
+    half = near.shape[0] // 2
+    keep = lax.dynamic_slice_in_dim(near, far_idx * half, half, 0)
+    send = lax.dynamic_slice_in_dim(near, (1 - far_idx) * half, half, 0)
+    got = lax.ppermute(send, FAR_LAST, perm=[(0, 1), (1, 0)])
+    projected = (keep.astype(jnp.float32) + got.astype(jnp.float32)).astype(jnp.bfloat16)
     mixed = projected[None]
     wanted = dp_idx * REQS + jnp.arange(REQS)
     take_hot = jnp.any(cache_slot[:, :, None] == wanted[None, None, :], axis=1).astype(jnp.float32)

time: 277 us -> 266 us (0.960)
  blocking collectives: 56.3 us -> 21.6 us
  starting transfers between devices: 0.3 us -> 13.3 us
  waiting for transfers between devices: 88.7 us -> 93.6 us
  other arithmetic: 22.3 us -> 26 us
  local copies, waits for them, and re-layouts: 47.3 us -> 50.7 us
    reduce_scatter x1 -> x0, waiting for transfers between devices: 55.6 us -> none  [local(): lax.psum_scatter(near, FAR_LAST, scatter_dimension=0, tiled=True)]
    ppermute x0 -> x1, waiting for transfers between devices: none -> 36.3 us  [local(): got = lax.ppermute(send, FAR_LAST, perm=[(0, 1), (1, 0)])]
    all_to_all x1 -> x0, blocking collectives: 34.8 us -> none  [local(): lax.all_to_all(outbound.astype(jnp.bfloat16), 'dp', split_axis=0, concat_...]
    all_to_all x0 -> x1, waiting for transfers between devices: none -> 26.5 us  [local(): lax.all_to_all(outbound.astype(jnp.bfloat16), 'dp', split_axis=0, concat_...]
    all_to_all x0 -> x1, starting transfers between devices: none -> 8.44 us  [local(): lax.all_to_all(outbound.astype(jnp.bfloat16), 'dp', split_axis=0, concat_...]
    ppermute x0 -> x1, starting transfers between devices: none -> 4.83 us  [local(): got = lax.ppermute(send, FAR_LAST, perm=[(0, 1), (1, 0)])]
  transfers between devices with their start and end apart: 2 -> 3, of which waited for: 2 -> 3; matrix products, arithmetic and copies ran while one was open for 8% -> 9% of each run, Pallas kernels for 0% -> 0%
where the time goes in v5:
time: 266 us; the launch traced here: 265 us
  waiting for transfers between devices  93.6 us (35%)
  local copies, waits for them, and re-layouts  50.7 us (19%)
  matrix products  45 us (17%)
  other arithmetic  26 us (10%)
  blocking collectives  21.6 us (8%)
  between operations  14.4 us (5%)
  starting transfers between devices  13.3 us (5%)
    ppermute x1, waiting for transfers between devices, local(): got = lax.ppermute(send, FAR_LAST, perm=[(0, 1), (1, 0)])  36.3 us
    reduce_scatter x1, waiting for transfers between devices, local(): lax.psum_scatter(partial, NEAR_FIRST, scatter_dimension=0, tiled=True)  30.8 us
    all_to_all x1, waiting for transfers between devices, local(): lax.all_to_all(outbound.astype(jnp.bfloat16), 'dp', split_axis=0, concat_...  26.5 us
    all_gather x1, blocking collectives, local(): group_stat = lax.all_gather(sum_sq, GROUP_MATES, tiled=True)  21.6 us
    dot_general x4, matrix products, split_einsum(): jnp.einsum(form, lower, narrow, preferred_element_type=jnp.float32)  14.1 us
    unnamed x62, local copies, waits for them, and re-layouts  13 us
    dot_general x1, matrix products, local(): jnp.dot(reordered, out_weight, preferred_element_type=jnp.float32)  12.6 us
    dot_general x4, matrix products, split_einsum(): first = jnp.einsum(form, upper, narrow, preferred_element_type=jnp.float32)  9.09 us
  transfers between devices with their start and end apart: 3, of which 3 were waited for; matrix products, arithmetic and copies ran while one was open for 9% of the time, Pallas kernels for 0%

profile of v5, /device:TPU:32, one launch (start us, length us, event | category | flops | bytes accessed | tf_op | source)
XLA Modules:
  0.0 264.6 jit_solution(3308803690519148081)
XLA Ops:
  7.2 0.5 broadcast.237
  7.8 1.4 reduce.9
  9.3 0.7 neg.23
  10.0 0.9 multiply_bitcast_fusion
  10.9 2.0 reduce-window.6
  12.9 0.2 slice_reduce_fusion
  13.1 0.2 reduce-window.9
  13.3 0.6 copy-done.8
  14.3 0.9 dynamic-slice_reduce_fusion
  15.2 0.5 and_select_fusion
  15.7 0.7 compare_convert_fusion
  16.4 0.7 fusion.51
  17.0 0.6 copy.328
  17.7 0.6 iota_compare_fusion
  18.3 3.3 %copy.253 = bf16[56,8,8,256]{3,2,1,0:T(8,128)(2,1)} copy(bf16[56,8,8,256]{3,1,2,0:T(8,128)(2,1)} %bitcast.156) | data formatting | bytes 3670016
  21.7 0.1 copy.246
  21.8 0.8 reduce.3
  22.6 0.1 copy.247
  22.7 2.6 constant_dynamic-slice_fusion.1
  25.3 1.2 copy.243
  26.6 1.0 copy.193
  27.6 1.3 compare_and_fusion
  29.0 1.5 fusion.39
  30.5 0.7 exponential_multiply_fusion
  31.2 6.7 %fusion.4 = f32[8,7,256,64]{2,3,1,0:T(8,128)} fusion(f32[8,256,256]{2,1,0:T(8,128)S(1)} %fusion.39, f32[8,7,256]{2,1,0:T(8,128)S(1)} %get-tuple-element.10, f32[8,7,256]{2,1,0:T(8,128)S(1)} %copy.193, pred[8,256,256]{2,1,0:T(8,128)(4,1)S(1)} %compare_and_fusion, bf16[8,256,7,64]{1,0,3,2:T(8,128)(2,1)S(1)} %bitcast.150), kind=kOutput, calls=%fused_computation.7 | convolution fusion | flops 488112128 | bytes 8241152 | tf_op jit(solution)/shard_map/bhts,bshp->bthp/dot_general | solution.py:30
  37.9 6.9 %fusion.1 = f32[8,7,256,64]{2,3,1,0:T(8,128)} fusion(f32[8,256,256]{2,1,0:T(8,128)S(1)} %fusion.39, f32[8,7,256]{2,1,0:T(8,128)S(1)} %get-tuple-element.10, f32[8,7,256]{2,1,0:T(8,128)S(1)} %copy.193, pred[8,256,256]{2,1,0:T(8,128)(4,1)S(1)} %compare_and_fusion, bf16[8,256,7,64]{1,0,3,2:T(8,128)(2,1)S(1)} %bitcast.151), kind=kOutput, calls=%fused_computation.5 | convolution fusion | flops 499122176 | bytes 8241152 | tf_op jit(solution)/shard_map/bhts,bshp->bthp/dot_general | solution.py:31
  44.7 2.3 convert_element_type.197
  47.0 5.7 %reshape.356 = f32[2,2,2,2,128,448]{4,3,2,1,0,5:T(2,128)} reshape(bf16[1,2048,448]{1,2,0:T(8,128)(2,1)} %param.12) | data formatting | bytes 5505024 | tf_op jit(solution)/shard_map/convert_element_type | solution.py:120
  52.8 3.9 %copy.254 = f32[56,8,8,256]{3,2,1,0:T(8,128)S(1)} copy(f32[56,8,8,256]{3,1,2,0:T(8,128)} %bitcast.148) | data formatting | bytes 7340032
  56.7 0.7 fusion.18
  57.4 0.6 fusion.28
  58.1 1.8 multiply_reduce_fusion
  59.9 0.6 fusion.37
  60.6 0.2 copy-done.14
  60.8 1.2 copy-done.22
  62.0 4.5 %multiply_reduce_fusion.1 = (f32[8,256]{1,0:T(8,128)S(1)}, f32[8,256,7,64]{1,3,2,0:T(8,128)}) fusion(f32[8,256,7,64]{1,0,3,2:T(8,128)S(1)} %bitcast.161, bf16[8,256,7,64]{1,0,3,2:T(8,128)(2,1)S(1)} %bitcast.154, f32[7]{0:T(128)S(1)} %copy-done.21, f32[8,256,7]{1,2,0:T(8,128)S(1)} %copy-done.14, f32[8,256,7,64]{1,3,2,0:T(8,128)S(1)} %fusion.37, ...), kind=kOutput, calls=%fused_computation.24 | convolution fusion | flops 131201024 | bytes 21430300 | tf_op jit(solution)/shard_map/bhpn,btn->bthp/dot_general | solution.py:31
  66.5 21.6 %all_gather.3 = f32[16384]{0:T(1024)} all-gather(f32[2048]{0:T(1024)S(1)} %bitcast.185), channel_id=1, replica_groups=mesh['dp'=16,'head_group'=2,'y_rest'=2,'z_hi'=2,'core'=2] {'y_rest','z_h..., dimensions={0}, use_global_device_ids=true | all-gather | bytes 73728 | tf_op jit(solution)/shard_map/all_gather | solution.py:122
  88.1 0.9 reshape.351
  89.0 5.4 %reshape.350 = f32[2,2,2,2,128,448]{4,3,5,2,1,0:T(2,128)} reshape(f32[8,256,7,64]{1,3,2,0:T(8,128)} %get-tuple-element.14) | data formatting | bytes 7340032 | tf_op jit(solution)/shard_map/reshape | solution.py:97
  94.5 4.9 %fusion.27 = bf16[2,2,2,2,128,448]{4,5,2,3,1,0:T(8,128)(2,1)S(1)} fusion(f32[448]{0:T(512)S(1)} %copy-done.19, f32[2,2,2,2,128]{4,3,2,1,0:T(2,128)S(1)} %bitcast.186, f32[2,2,2,2,128,448]{4,3,2,1,0,5:T(2,128)} %reshape.356, f32[2,2,2,2,128,448]{4,3,5,2,1,0:T(2,128)} %reshape.350), kind=kLoop, calls=%fused_computation.38 | loop fusion | flops 7340032 | bytes 9185024 | tf_op jit(solution)/shard_map/transpose | solution.py:131
  99.3 3.1 %copy.222 = bf16[2,2,2,2,128,448]{4,3,2,1,0,5:T(2,128)(2,1)} copy(bf16[2,2,2,2,128,448]{4,5,2,3,1,0:T(8,128)(2,1)S(1)} %fusion.27) | data formatting | bytes 3670016 | tf_op jit(solution)/shard_map/transpose | solution.py:131
  102.5 5.3 %reshape.352 = bf16[2048,448]{0,1:T(8,128)(2,1)} reshape(bf16[2,2,2,2,128,448]{4,3,2,1,0,5:T(2,128)(2,1)} %copy.222) | data formatting | bytes 3670016 | tf_op jit(solution)/shard_map/reshape | solution.py:132
  107.7 12.6 %convolution_convert_fusion = bf16[2048,3584]{1,0:T(8,128)(2,1)} fusion(bf16[2048,448]{0,1:T(8,128)(2,1)} %reshape.352, bf16[448,3584]{1,0:T(8,128)(2,1)S(1)} %copy-done), kind=kOutput, calls=%fused_computation | convolution fusion | flops 6584008704 | bytes 19726336 | tf_op jit(solution)/shard_map/dot_general | solution.py:134
  120.4 0.7 copy-done.13
  121.2 0.2 fusion.47
  121.3 1.1 fusion.17
  122.5 0.2 broadcast_multiply_fusion
  122.7 0.7 fusion.12
  123.4 1.1 fusion.58
  124.6 2.1 convolution_add_fusion
  126.6 2.6 reshape.353
  129.3 3.1 %copy.324 = f32[7,64,8,64]{3,1,0,2:T(8,128)} copy(f32[7,64,8,64]{3,2,1,0:T(8,128)} %reshape.353) | data formatting | bytes 1835008 | tf_op jit(solution)/shard_map/reshape | solution.py:116
  132.3 3.0 %reshape.354 = f32[8,28672]{1,0:T(8,128)} reshape(f32[8,7,64,64]{3,2,1,0:T(8,128)} %bitcast.155) | data formatting | bytes 1835008 | tf_op jit(solution)/shard_map/reshape | solution.py:118
  135.3 2.3 convolution_convert_fusion.1
  137.6 1.5 copy.224
  139.1 8.4 %all-to-all-start = ((bf16[16,7,4096]{2,1,0:T(8,128)(2,1)}), bf16[16,7,4096]{2,1,0:T(8,128)(2,1)}, u32[]{:S(2)}, u32[]{:S(2)}) async-start(bf16[16,7,4096]{2,1,0:T(8,128)(2,1)} %copy.224), calls=%async_computation.1 | async-start | bytes 2097152 | tf_op jit(solution)/shard_map/all_to_all | solution.py:144
  147.5 26.5 %all-to-all-done = bf16[16,7,4096]{2,1,0:T(8,128)(2,1)} async-done(((bf16[16,7,4096]{2,1,0:T(8,128)(2,1)}), bf16[16,7,4096]{2,1,0:T(8,128)(2,1)}, u32[]{:S(2)}, u32[]{:S(2)}) %all-to-all-start) | async-done | bytes 917536 | tf_op jit(solution)/shard_map/all_to_all | solution.py:144
  174.0 2.8 %convert_element_type.193 = f32[16,7,4096]{2,1,0:T(8,128)} convert(bf16[16,7,4096]{2,1,0:T(8,128)(2,1)} %all-to-all-done) | non-fusion elementwise | flops 458752 | bytes 2752512 | tf_op jit(solution)/shard_map/convert_element_type | solution.py:146
  176.8 30.8 %reduce-scatter.2.cloned.1.call-done = bf16[256,3584]{1,0:T(8,128)(2,1)} async-done(((bf16[2048,3584]{1,0:T(8,128)(2,1)}), bf16[256,3584]{1,0:T(8,128)(2,1)}) %reduce-scatter.2.cloned.1.call-update) | async-done | bytes 1835024 | tf_op jit(solution)/shard_map/reduce_scatter | solution.py:135
  207.6 2.2 constant_dynamic-slice_fusion
  209.7 4.8 %collective-permute-start = (bf16[128,3584]{1,0:T(8,128)(2,1)}, bf16[128,3584]{1,0:T(8,128)(2,1)}, u32[]{:S(2)}, u32[]{:S(2)}) collective-permute-start(bf16[128,3584]{1,0:T(8,128)(2,1)} %constant_dynamic-slice_fusion), channel_id=1, source_target_pairs={{0,2},{2,0},{1,3},{3,1},{4,6},{6,4},{5,7},{7,5},{8,10},{10,8},{9,1... | collective-permute-start | bytes 2752520 | tf_op jit(solution)/shard_map/ppermute | solution.py:152
  214.7 4.2 %fusion.20 = f32[8,7,4096]{2,0,1:T(8,128)} fusion(pred[16,8]{0,1:T(8,128)(4,1)S(1)} %compare_reduce_fusion, f32[2,8,7,4096]{3,2,1,0:T(8,128)} %bitcast.149), kind=kOutput, calls=%fused_computation.30 | convolution fusion | flops 44040192 | bytes 2752640 | tf_op jit(solution)/shard_map/dot_general | solution.py:157
  218.8 36.3 %collective-permute-done = bf16[128,3584]{1,0:T(8,128)(2,1)} collective-permute-done((bf16[128,3584]{1,0:T(8,128)(2,1)}, bf16[128,3584]{1,0:T(8,128)(2,1)}, u32[]{:S(2)}, u32[]{:S(2)}) %collective-permute-start) | collective-permute-done | bytes 917536 | tf_op jit(solution)/shard_map/ppermute | solution.py:152
  255.2 2.6 fusion.35
  (68 shorter events, 1.2 us)
Async XLA Ops:
  7.2 100.6 %copy-start = (bf16[448,3584]{1,0:T(8,128)(2,1)S(1)}, bf16[448,3584]{1,0:T(8,128)(2,1)}, u32[]{:S(2)}) copy-start(bf16[448,3584]{1,0:T(8,128)(2,1)} %param.19) | copy-start | bytes 9633796
  7.2 14.6 %copy-start.12 = (f32[1,2048,7]{1,0,2:T(1,128)S(1)}, f32[1,2048,7]{1,0,2:T(1,128)}, u32[]{:S(2)}) copy-start(f32[1,2048,7]{1,0,2:T(1,128)} %param.15) | copy-start | bytes 172036
  7.2 200.4 %reduce-scatter.2.cloned.1.call-start = ((), (), s32[]{:S(2)}) async-start(), calls=%async_computation.2 | async-start | bytes 16515072 | tf_op jit(solution)/shard_map/reduce_scatter | solution.py:135
  13.3 0.6 copy-start.8
  26.5 3.9 %copy-start.11 = (f32[2048,7]{0,1:T(8,128)S(1)}, f32[2048,7]{0,1:T(8,128)}, u32[]{:S(2)}) copy-start(f32[2048,7]{0,1:T(8,128)} %reduce.3) | copy-start | bytes 172036
  26.5 3.9 %copy-start.15 = (f32[8,256]{1,0:T(8,128)S(1)}, f32[8,256]{1,0:T(8,128)}, u32[]{:S(2)}) copy-start(f32[8,256]{1,0:T(8,128)} %get-tuple-element.11) | copy-start | bytes 24580
  26.5 3.9 %copy-start.16 = (f32[8,256]{1,0:T(8,128)S(1)}, f32[8,256]{1,0:T(8,128)}, u32[]{:S(2)}) copy-start(f32[8,256]{1,0:T(8,128)} %get-tuple-element.12) | copy-start | bytes 24580
  26.5 4.7 %copy-start.1 = (bf16[56,8,8,256]{3,2,1,0:T(8,128)(2,1)S(1)}, bf16[56,8,8,256]{3,2,1,0:T(8,128)(2,1)}, u32[]{:S(2)}) copy-start(bf16[56,8,8,256]{3,2,1,0:T(8,128)(2,1)} %copy.253) | copy-start | bytes 5505028
  26.6 2.3 copy-start.6
  37.9 6.9 %copy-start.4 = (bf16[1,2048,448]{1,2,0:T(8,128)(2,1)S(1)}, bf16[1,2048,448]{1,2,0:T(8,128)(2,1)}, u32[]{:S(2)}) copy-start(bf16[1,2048,448]{1,2,0:T(8,128)(2,1)} %param.12) | copy-start | bytes 5505028
  52.8 3.9 %copy-start.2 = (bf16[56,8,8,256]{3,2,1,0:T(8,128)(2,1)S(1)}, bf16[56,8,8,256]{3,2,1,0:T(8,128)(2,1)}, u32[]{:S(2)}) copy-start(bf16[56,8,8,256]{3,2,1,0:T(8,128)(2,1)} %copy.253) | copy-start | bytes 5505028
  52.8 3.9 %copy-start.7 = (bf16[8,8,8,256]{3,2,1,0:T(8,128)(2,1)S(1)}, bf16[8,8,8,256]{3,2,1,0:T(8,128)(2,1)}, u32[]{:S(2)}) copy-start(bf16[8,8,8,256]{3,2,1,0:T(8,128)(2,1)} %copy-done.6) | copy-start | bytes 786436
  52.8 3.9 %copy-start.10 = (f32[8,256,7]{1,2,0:T(8,128)S(1)}, f32[8,256,7]{1,2,0:T(8,128)}, u32[]{:S(2)}) copy-start(f32[8,256,7]{1,2,0:T(8,128)} %get-tuple-element.9) | copy-start | bytes 172036
  57.3 0.7 copy-start.18
  57.3 2.6 copy-start.5
  58.1 2.5 copy-start.23
  59.9 0.9 copy-start.14
  59.9 0.9 copy-start.21
  59.9 2.1 copy-start.22
  89.0 5.4 %copy-start.19 = (f32[448]{0:T(512)S(1)}, f32[448]{0:T(512)}, u32[]{:S(2)}) copy-start(f32[448]{0:T(512)} %param.18) | copy-start | bytes 5380
  120.3 0.7 copy-start.13
  120.3 0.8 copy-start.9
  120.3 2.3 copy-start.3
  129.3 6.1 %copy-start.20 = (s32[8]{0:T(128)S(1)}, s32[8]{0:T(128)}, u32[]{:S(2)}) copy-start(s32[8]{0:T(128)} %get-tuple-element.15) | copy-start | bytes 100
  139.1 75.5 %copy-start.17 = (s32[16,8]{0,1:T(8,128)S(1)}, s32[16,8]{0,1:T(8,128)}, u32[]{:S(2)}) copy-start(s32[16,8]{0,1:T(8,128)} %param.21) | copy-start | bytes 1540
  139.1 34.9 %all-to-all-start = ((bf16[16,7,4096]{2,1,0:T(8,128)(2,1)}), bf16[16,7,4096]{2,1,0:T(8,128)(2,1)}, u32[]{:S(2)}, u32[]{:S(2)}) async-start(bf16[16,7,4096]{2,1,0:T(8,128)(2,1)} %copy.224), calls=%async_computation.1 | async-start | bytes 2097152 | tf_op jit(solution)/shard_map/all_to_all | solution.py:144
  209.7 45.4 %collective-permute-start = (bf16[128,3584]{1,0:T(8,128)(2,1)}, bf16[128,3584]{1,0:T(8,128)(2,1)}, u32[]{:S(2)}, u32[]{:S(2)}) collective-permute-start(bf16[128,3584]{1,0:T(8,128)(2,1)} %constant_dynamic-slice_fusion), channel_id=1, source_target_pairs={{0,2},{2,0},{1,3},{3,1},{4,6},{6,4},{5,7},{7,5},{8,10},{10,8},{9,1... | collective-permute-start | bytes 2752520 | tf_op jit(solution)/shard_map/ppermute | solution.py:152
Sparse Core Ops, SparseCore 0:
  120.5 87.0 reduce-scatter.1
